TPU v7x, 256 devices: a whole 4x4x8 slice. The times are simulated.
256 devices in a mesh: keys: 32 (over x, y, core), vocab: 8 (over z).
Axes of the slice: x: 4, y: 4, z: 8, core: 2. Of those that a mesh axis runs over, the one named last changes fastest.
Arguments:
- hidden: bfloat16 [1024, 4096], P(('keys', 'vocab')), may hold values from -24 to 24
- queries: bfloat16 [1024, 1024], P(('keys', 'vocab')), may hold values from -24 to 24
- probes: int32 [1024, 64], P(('keys', 'vocab')), may hold values from 0 to 95, as said below
- counts: int32 [1024], P(('keys', 'vocab')), may hold values from 16 to 64
- block_slot: int32 [96], replicated, may hold values from 0 to 95, as said below
- key_store: bfloat16 [96, 512, 1024], P('keys'), may hold values from -7 to 7
- stored_next_tokens: int32 [96, 512], replicated, may hold values from 0 to 128255
- head_weight: bfloat16 [4096, 128256], P(None, ('keys', 'vocab'))
Outputs:
- mixed_logp: float32 [1024, 128256], P(('keys', 'vocab'))
Inputs may be any that keep to these rules, and one draw needn't show every extreme that they name: `probes`: the 64 ids of a row are distinct block ids; only the first counts of them are probed. At most 2 of a row's 64 ids map through block_slot to slots held by one keys index. `block_slot`: A permutation of the slots; slot s lies in the part of the key store held by keys index s // 3.
All inputs are finite; a program needn't handle non-finite values.
Results may differ from a plain program's by a relative error of at most 0.0003.
Values may be sent and summed in bfloat16 or wider, within the bound.
No kernel may reach another device: no remote copies, remote signals or barrier semaphores. Data moves between devices by JAX's collectives and lax.ppermute only.
A program may use at most 128 MiB of HBM per device.

v0:
```python
import math

import jax
import jax.numpy as jnp
from jax import lax
from jax.sharding import PartitionSpec as P

LAMBDA = 0.25
SMOOTH = 0.1


def joined(part, axis, combine):
    gathered = jax.tree.map(lambda a: lax.all_gather(a, axis), part)

    def take(source):
        return jax.tree.map(lambda a: lax.dynamic_index_in_dim(a, source, 0, False), gathered)

    return lax.fori_loop(
        1, lax.axis_size(axis), lambda source, state: combine(state, take(source)), take(0)
    )


def merge_totals(earlier, later):
    row_peak = jnp.maximum(earlier[0], later[0])
    combined = earlier[1] * jnp.exp(earlier[0] - row_peak) + later[1] * jnp.exp(later[0] - row_peak)
    return (row_peak, combined)


def pick_blocks(table, index_row):
    return table[index_row]


def shards(hidden, queries, probes, counts, block_slot, key_store, stored_next_tokens, head_weight):
    rows_dev = hidden.shape[0]
    piece_cols = head_weight.shape[1]
    local_blocks = key_store.shape[0]
    block_len = key_store.shape[1]
    key_width = key_store.shape[2]
    key_count = lax.axis_size("keys")
    vocab_count = lax.axis_size("vocab")
    probe_cap = probes.shape[1]
    logits = jnp.dot(
        lax.all_gather(hidden, ("keys", "vocab"), axis=0, tiled=True),
        head_weight,
        preferred_element_type=jnp.float32,
    )
    local_peak = jnp.max(logits, axis=1)
    local_sum = jnp.sum(jnp.exp(logits - local_peak[:, None]), axis=1)
    row_peak, row_sum = joined((local_peak, local_sum), ("keys", "vocab"), merge_totals)
    logits = logits - (row_peak + jnp.log(row_sum))[:, None]
    blocks = logits.reshape(key_count, vocab_count, rows_dev, 1, 1, piece_cols)
    arrived = lax.all_to_all(
        lax.all_to_all(blocks, "keys", split_axis=0, concat_axis=3, tiled=True),
        "vocab",
        split_axis=1,
        concat_axis=4,
        tiled=True,
    )
    whole_rows = arrived.reshape(rows_dev, key_count * vocab_count * piece_cols)
    group_queries = lax.all_gather(queries, "keys", axis=0, tiled=True)
    flat_keys = key_store.reshape(local_blocks * block_len, key_width)
    key_norms = jnp.sum(jnp.square(flat_keys.astype(jnp.float32)), axis=1)
    query_norms = jnp.sum(jnp.square(group_queries.astype(jnp.float32)), axis=1)
    inner_prod = lax.dot_general(
        group_queries, flat_keys, (((1,), (1,)), ((), ())), preferred_element_type=jnp.float32
    )
    score_scale = 0.5 / math.sqrt(key_width)
    scores = -(query_norms[:, None] + key_norms[None, :] - 2.0 * inner_prod) * score_scale
    slot_ids = block_slot[probes]
    outgoing = scores.reshape(key_count, rows_dev, local_blocks, block_len)
    incoming = lax.all_to_all(outgoing, "keys", split_axis=0, concat_axis=2, tiled=True)
    every_slot = incoming.reshape(rows_dev, key_count * local_blocks, block_len)
    chosen = jax.vmap(pick_blocks)(every_slot, slot_ids)
    live_mask = (jnp.arange(probe_cap, dtype=jnp.int32)[None, :] < counts[:, None])[:, :, None]
    best_score = jnp.max(jnp.where(live_mask, chosen, -jnp.inf), axis=(1, 2), keepdims=True)
    raised = jnp.where(live_mask, jnp.exp(chosen - best_score), 0.0)
    weights = raised / jnp.sum(raised, axis=(1, 2), keepdims=True)
    tokens = stored_next_tokens[slot_ids]
    row_ids = jnp.broadcast_to(jnp.arange(rows_dev, dtype=jnp.int32)[:, None, None], tokens.shape)
    vocab_size = whole_rows.shape[1]
    knn_mass = jnp.zeros((rows_dev, vocab_size), jnp.float32).at[row_ids, tokens].add(weights)
    return jnp.log(
        LAMBDA * (knn_mass + SMOOTH / vocab_size) / (1.0 + SMOOTH)
        + (1.0 - LAMBDA) * jnp.exp(whole_rows)
    )


def solution(mesh):
    placed = (
        P(("keys", "vocab"), None),
        P(("keys", "vocab"), None),
        P(("keys", "vocab"), None),
        P(("keys", "vocab")),
        P(),
        P("keys", None, None),
        P(),
        P(None, ("keys", "vocab")),
    )
    return jax.shard_map(
        shards, mesh=mesh, in_specs=placed, out_specs=P(("keys", "vocab"), None), check_vma=False
    )
```

profile of v0, /device:TPU:1, one launch (start us, length us, event | category | flops | bytes accessed | tf_op | source)
XLA Modules:
  0.0 1358.9 jit_solution(2815163394601035959)
XLA Ops:
  7.3 125.8 %all-gather.12.cloned.1.call-done = bf16[256,4,4096]{2,1,0:T(4,128)(2,1)} async-done(((bf16[1,4,4096]{2,1,0:T(4,128)(2,1)}), bf16[256,4,4096]{2,1,0:T(4,128)(2,1)}) %all-gather.12.cloned.1.call-update) | async-done | bytes 8388624 | tf_op jit(solution)/shard_map/all_gather | solution.py:43
  133.1 12.5 reshape.128
  145.6 10.5 fusion.7
  156.1 2.5 exponential_reduce_fusion
  159.4 27.1 %all-gather.2 = bf16[32,4,1024]{2,1,0:T(4,128)(2,1)} all-gather(bf16[1,4,1024]{2,1,0:T(4,128)(2,1)S(1)} %bitcast.55), channel_id=1, replica_groups=mesh['keys'=32,'vocab'=8] {'keys'}, dimensions={0}, use_global_device_ids=true | all-gather | bytes 270336 | tf_op jit(solution)/shard_map/all_gather | solution.py:60
  186.5 1.7 reshape.126
  188.9 1.1 multiply_reduce_fusion.2
  190.0 3.0 fusion.2
  193.0 1.7 reshape.77
  194.8 1.2 copy.18
  196.0 4.4 all-to-all-start
  200.4 59.7 %all-gather.10.cloned.1.call-done = f32[262144]{0:T(1024)} async-done(((f32[1024]{0:T(1024)}), f32[262144]{0:T(1024)}) %all-gather.10.cloned.1.call-update) | async-done | bytes 1048592 | tf_op jit(solution)/shard_map/all_gather | solution.py:13
  260.2 2.4 reshape.115
  262.6 103.3 %all-gather.8.cloned.1.call-done = f32[262144]{0:T(1024)} async-done(((f32[1024]{0:T(1024)}), f32[262144]{0:T(1024)}) %all-gather.8.cloned.1.call-update) | async-done | bytes 1048592 | tf_op jit(solution)/shard_map/all_gather | solution.py:13
  365.9 2.4 reshape.114
  368.3 211.2 %while.17 = (s32[]{:T(128)}, f32[1024]{0:T(1024)S(1)}, f32[1024]{0:T(1024)S(1)}, f32[256,1024]{1,0:T(8,128)}, f32[256,1024]{1,0:T(8,128)}, /*index=5*/s32[]{:T(128)}, s32[]{:T(128)}, s32[]{:T(128)}) while((s32[]{:T(128)}, f32[1024]{0:T(1024)S(1)}, f32[1024]{0:T(1024)S(1)}, f32[256,1024]{1,0:T(8,128)}, f32[256,1024]{1,0:T(8,128)}, ...), condition=%wide.region_8.9_spmd, body=%wide.region_7.8_spmd.sunk | while | flops 6149 | bytes 41091 | solution.py:18
  579.6 1.6 broadcast_subtract_fusion
  581.1 1.9 copy.20
  583.1 1.7 reshape.79
  584.8 7.3 all-to-all-start.1
  592.1 1.9 gather_fusion
  594.2 1.0 gather_fusion.1
  596.8 2.1 gather_fusion.2
  599.8 683.5 %scatter_custom_fusion = f32[513024]{0:T(1024)} fusion(s32[131072]{0:T(1024)S(1)} %bitcast.50, f32[131072]{0:T(1024)S(1)} %bitcast.51, f32[]{:T(128)} %constant.63.clone.1), kind=kCustom, calls=%fused_computation.21 | custom fusion | flops 131072 | bytes 2052100
  1283.2 3.3 copy.22
  1286.6 4.6 all-to-all-start.2
  1291.2 3.1 broadcast_multiply_fusion
  1294.2 3.8 reshape.85
  1298.1 44.8 %all-to-all-done.2 = f32[1,8,4,32,1,501]{5,2,3,4,0,1:T(4,128)S(1)} async-done(((f32[1,8,4,32,1,501]{5,2,3,4,0,1:T(4,128)}), f32[1,8,4,32,1,501]{5,2,3,4,0,1:T(4,128)S(1)}, u32[]{:S(2)}, u32[]{:S(2)}) %all-to-all-start.2) | async-done | bytes 2052128 | tf_op jit(solution)/shard_map/all_to_all | solution.py:52
  1343.5 1.2 copy.23
  1344.7 3.5 mul.57
  1348.2 4.2 add_log_fusion
  (566 shorter events, 209.6 us)
Async XLA Ops:
  6.5 587.7 %copy-start = (s32[96,512]{1,0:T(8,128)S(1)}, s32[96,512]{1,0:T(8,128)}, u32[]{:S(2)}) copy-start(s32[96,512]{1,0:T(8,128)} %param.16) | copy-start | bytes 589828
  6.5 126.5 %all-gather.12.cloned.1.call-start = ((), (), s32[]{:S(2)}) async-start(), calls=%async_computation.5 | async-start | bytes 8421376 | tf_op jit(solution)/shard_map/all_gather | solution.py:43
  7.3 252.9 %all-gather.10.cloned.1.call-start = ((), (), s32[]{:S(2)}) async-start(), calls=%async_computation.4 | async-start | bytes 1052672 | tf_op jit(solution)/shard_map/all_gather | solution.py:13
  145.6 42.6 %copy-start.2 = (bf16[3,512,1024]{2,1,0:T(8,128)(2,1)S(1)}, bf16[3,512,1024]{2,1,0:T(8,128)(2,1)}, u32[]{:S(2)}) copy-start(bf16[3,512,1024]{2,1,0:T(8,128)(2,1)} %param.15) | copy-start | bytes 9437188
  156.1 2.6 copy-start.4
  156.1 3.2 copy-start.5
  158.6 207.3 %all-gather.8.cloned.1.call-start = ((), (), s32[]{:S(2)}) async-start(), calls=%async_computation.3 | async-start | bytes 1052672 | tf_op jit(solution)/shard_map/all_gather | solution.py:13
  194.8 5.6 copy-start.6
  196.0 388.8 %all-to-all-start = ((f32[32,4,3,512]{3,1,2,0:T(4,128)}), f32[32,4,3,512]{3,1,2,0:T(4,128)S(1)}, u32[]{:S(2)}, u32[]{:S(2)}) async-start(f32[32,4,3,512]{3,1,2,0:T(4,128)} %copy.18), calls=%async_computation | async-start | bytes 1572864 | tf_op jit(solution)/shard_map/all_to_all | solution.py:71
  200.4 379.1 %copy-start.3 = (f32[1024,501]{0,1:T(8,128)S(1)}, f32[1024,501]{0,1:T(8,128)}, u32[]{:S(2)}) copy-start(f32[1024,501]{0,1:T(8,128)} %get-tuple-element.157) | copy-start | bytes 6156292
  260.2 108.2 %slice-start = ((f32[262144]{0:T(1024)}), f32[1024]{0:T(1024)S(1)}, s32[]{:S(2)}) async-start(f32[262144]{0:T(1024)} %all-gather.10.cloned.1.call-done), calls=%async_computation.6 | async-start | bytes 8192 | tf_op jit(solution)/shard_map/jit(dynamic_index_in_dim)/dynamic_slice | solution.py:16
  365.9 2.4 slice-start.1
  584.8 7.3 copy-start.1
  584.8 698.5 %all-to-all-start.1 = ((f32[32,8,4,1,1,501]{5,2,1,4,3,0:T(4,128)}), f32[32,8,4,1,1,501]{5,2,1,4,3,0:T(4,128)}, u32[]{:S(2)}, u32[]{:S(2)}) async-start(f32[32,8,4,1,1,501]{5,2,1,4,3,0:T(4,128)} %bitcast.10), calls=%async_computation.1 | async-start | bytes 4194304 | tf_op jit(solution)/shard_map/all_to_all | solution.py:53
  594.2 1.1 copy-start.8
  595.2 0.7 copy-start.7
  595.9 0.7 copy-start.9
  1286.6 56.2 %all-to-all-start.2 = ((f32[1,8,4,32,1,501]{5,2,3,4,0,1:T(4,128)}), f32[1,8,4,32,1,501]{5,2,3,4,0,1:T(4,128)S(1)}, u32[]{:S(2)}, u32[]{:S(2)}) async-start(f32[1,8,4,32,1,501]{5,2,3,4,0,1:T(4,128)} %copy.22), calls=%async_computation.2 | async-start | bytes 4194304 | tf_op jit(solution)/shard_map/all_to_all | solution.py:52
Sparse Core Ops, SparseCore 0:
  11.0 121.9 all-gather.11
  158.8 101.3 all-gather.9
  263.9 101.9 all-gather.7
where the time goes:
time: 1380 us; the launch traced here: 1360 us
  other arithmetic  701 us (51%)
  waiting for transfers between devices  335 us (24%)
  local copies, waits for them, and re-layouts  245 us (18%)
  blocking collectives  27.1 us (2%)
  starting transfers between devices  16.3 us (1%)
    unnamed x4, other arithmetic  684 us
    dynamic_slice x259, local copies, waits for them, and re-layouts, take(): lax.dynamic_index_in_dim(a, source, 0, False)  201 us
    all_gather x2, waiting for transfers between devices, joined(): gathered = jax.tree.map(lambda a: lax.all_gather(a, axis), part)  163 us
    all_gather x1, waiting for transfers between devices, shards(): lax.all_gather(hidden, ('keys', 'vocab'), axis=0, tiled=True)  126 us
    all_to_all x1, waiting for transfers between devices, shards(): lax.all_to_all(lax.all_to_all(blocks, 'keys', split_axis=0, concat_axis=3...  44.8 us
  transfers between devices with their start and end apart: 6, of which 4 were waited for; matrix products, arithmetic and copies ran while one was open for 68% of the time, Pallas kernels for 0%

commit v1 on v0

v1 whole, which is shorter than its diff:
```python
import math

import jax
import jax.numpy as jnp
from jax import lax
from jax.experimental import pallas as pl
from jax.experimental.pallas import tpu as pltpu
from jax.sharding import PartitionSpec as P

LAMBDA = 0.25
SMOOTH = 0.1
LANES = 128


def code_range(vocab_size):
    floor = LAMBDA * (SMOOTH / vocab_size) / (1.0 + SMOOTH)
    return math.log(floor), math.log(floor + (1.0 - LAMBDA))


def knn_kernel(tok_ref, w_ref, out_ref, *accs):
    step = pl.program_id(0)

    @pl.when(step == 0)
    def _():
        for acc in accs:
            acc[...] = jnp.zeros_like(acc)

    lane = lax.broadcasted_iota(jnp.int32, (1, LANES), 1)

    def body(i, carry):
        for r, acc in enumerate(accs):
            token = tok_ref[r, i]
            weight = w_ref[r, i]
            row = token >> 7
            acc[pl.ds(row, 1), :] = acc[pl.ds(row, 1), :] + jnp.where(lane == (token & 127), weight, 0.0)
        return carry

    lax.fori_loop(0, tok_ref.shape[1], body, 0, unroll=8)

    @pl.when(step == pl.num_programs(0) - 1)
    def _():
        for r, acc in enumerate(accs):
            out_ref[r] = acc[...]


def knn_scatter(tokens, weights, vocab_size):
    rows, probes, block_len = tokens.shape
    tok = tokens.reshape(rows, probes * block_len)
    w = weights.reshape(rows, probes * block_len)
    lane_rows = vocab_size // LANES
    out = pl.pallas_call(
        knn_kernel,
        grid=(probes,),
        in_specs=[
            pl.BlockSpec((rows, block_len), lambda j: (0, j), memory_space=pltpu.SMEM),
            pl.BlockSpec((rows, block_len), lambda j: (0, j), memory_space=pltpu.SMEM),
        ],
        out_specs=pl.BlockSpec((rows, lane_rows, LANES), lambda j: (0, 0, 0)),
        out_shape=jax.ShapeDtypeStruct((rows, lane_rows, LANES), jnp.float32),
        scratch_shapes=[pltpu.VMEM((lane_rows, LANES), jnp.float32) for _ in range(rows)],
    )(tok, w)
    return out.reshape(rows, vocab_size)


def shards(hidden, queries, probes, counts, block_slot, key_store, stored_next_tokens, head_weight):
    rows_dev = hidden.shape[0]
    piece_cols = head_weight.shape[1]
    local_blocks = key_store.shape[0]
    block_len = key_store.shape[1]
    key_width = key_store.shape[2]
    key_count = lax.axis_size("keys")
    vocab_count = lax.axis_size("vocab")
    devices = key_count * vocab_count
    probe_cap = probes.shape[1]
    vocab_size = devices * piece_cols
    both = ("keys", "vocab")

    logits = jnp.dot(
        lax.all_gather(hidden, both, axis=0, tiled=True),
        head_weight,
        preferred_element_type=jnp.float32,
    )
    local_peak = jnp.max(logits, axis=1)
    row_peak = lax.pmax(local_peak, both)
    row_sum = lax.psum(jnp.sum(jnp.exp(logits - row_peak[:, None]), axis=1), both)
    log_probs = logits - (row_peak + jnp.log(row_sum))[:, None]
    floor = LAMBDA * (SMOOTH / vocab_size) / (1.0 + SMOOTH)
    lo, hi = code_range(vocab_size)
    base = jnp.log(floor + (1.0 - LAMBDA) * jnp.exp(log_probs))
    scale = 65535.0 / (hi - lo)
    code = (jnp.round((base - lo) * scale) - 32768.0).astype(jnp.int16)
    sent = code.reshape(devices, rows_dev, piece_cols)
    got = lax.all_to_all(sent, both, split_axis=0, concat_axis=0, tiled=True)
    got = got.reshape(devices, rows_dev, piece_cols).transpose(1, 0, 2).reshape(rows_dev, vocab_size)
    base_rows = (got.astype(jnp.float32) + 32768.0) * (1.0 / scale) + lo

    group_queries = lax.all_gather(queries, "keys", axis=0, tiled=True)
    flat_keys = key_store.reshape(local_blocks * block_len, key_width)
    key_norms = jnp.sum(jnp.square(flat_keys.astype(jnp.float32)), axis=1)
    query_norms = jnp.sum(jnp.square(group_queries.astype(jnp.float32)), axis=1)
    inner_prod = lax.dot_general(
        group_queries, flat_keys, (((1,), (1,)), ((), ())), preferred_element_type=jnp.float32
    )
    score_scale = 0.5 / math.sqrt(key_width)
    scores = -(query_norms[:, None] + key_norms[None, :] - 2.0 * inner_prod) * score_scale
    slot_ids = block_slot[probes]
    outgoing = scores.reshape(key_count, rows_dev, local_blocks, block_len)
    incoming = lax.all_to_all(outgoing, "keys", split_axis=0, concat_axis=2, tiled=True)
    every_slot = incoming.reshape(rows_dev, key_count * local_blocks, block_len)
    chosen = jnp.take_along_axis(every_slot, slot_ids[:, :, None], axis=1)
    live_mask = (jnp.arange(probe_cap, dtype=jnp.int32)[None, :] < counts[:, None])[:, :, None]
    best_score = jnp.max(jnp.where(live_mask, chosen, -jnp.inf), axis=(1, 2), keepdims=True)
    raised = jnp.where(live_mask, jnp.exp(chosen - best_score), 0.0)
    weights = raised / jnp.sum(raised, axis=(1, 2), keepdims=True)
    tokens = stored_next_tokens[slot_ids]
    knn_mass = knn_scatter(tokens, weights, vocab_size)
    mixed = jnp.log(jnp.exp(base_rows) + (LAMBDA / (1.0 + SMOOTH)) * knn_mass)
    return jnp.where(knn_mass > 0.0, mixed, base_rows)


def solution(mesh):
    placed = (
        P(("keys", "vocab"), None),
        P(("keys", "vocab"), None),
        P(("keys", "vocab"), None),
        P(("keys", "vocab")),
        P(),
        P("keys", None, None),
        P(),
        P(None, ("keys", "vocab")),
    )
    return jax.shard_map(
        shards, mesh=mesh, in_specs=placed, out_specs=P(("keys", "vocab"), None), check_vma=False
    )
```

time: 1380 us -> 624 us (0.45); the launches traced: 1360 us -> 623 us
  other arithmetic: 701 us -> 16.5 us
  Pallas kernels: 0 us -> 287 us
  waiting for transfers between devices: 335 us -> 72.4 us
  local copies, waits for them, and re-layouts: 245 us -> 31.9 us
  blocking collectives: 27.1 us -> 177 us
    unnamed x4 -> x2, other arithmetic: 684 us -> 3.51 us
    pallas_call x0 -> x1, Pallas kernels: none -> 287 us  [knn_scatter(): pl.pallas_call(knn_kernel, grid=(probes,), in_specs=[pl.BlockSpec((rows,...]
    all_gather x3 -> x1, waiting for transfers between devices: 289 us -> 62.2 us  [shards(): lax.all_gather(hidden, both, axis=0, tiled=True)]
    dynamic_slice x259 -> x0, local copies, waits for them, and re-layouts: 201 us -> none  [take(): lax.dynamic_index_in_dim(a, source, 0, False)]
    pmax x0 -> x1, blocking collectives: none -> 75.1 us  [shards(): row_peak = lax.pmax(local_peak, both)]
    psum x0 -> x1, blocking collectives: none -> 73.5 us  [shards(): lax.psum(jnp.sum(jnp.exp(logits - row_peak[:, None]), axis=1), both)]
    all_to_all x2 -> x1, waiting for transfers between devices: 44.8 us -> 0.01 us  [shards(): got = lax.all_to_all(sent, both, split_axis=0, concat_axis=0, tiled=True)]
  transfers between devices with their start and end apart: 6 -> 3, of which waited for: 4 -> 2; matrix products, arithmetic and copies ran while one was open for 68% -> 4% of each run, Pallas kernels for 0% -> 46%
where the time goes in v1:
time: 624 us; the launch traced here: 623 us
  Pallas kernels  287 us (46%)
  blocking collectives  177 us (28%)
  waiting for transfers between devices  72.4 us (12%)
  local copies, waits for them, and re-layouts  31.9 us (5%)
  other arithmetic  16.5 us (3%)
  between operations  13.6 us (2%)
  starting transfers between devices  13.1 us (2%)
  matrix products  11.2 us (2%)
    pallas_call x1, Pallas kernels, knn_scatter(): pl.pallas_call(knn_kernel, grid=(probes,), in_specs=[pl.BlockSpec((rows,...  287 us
    pmax x1, blocking collectives, shards(): row_peak = lax.pmax(local_peak, both)  75.1 us
    psum x1, blocking collectives, shards(): lax.psum(jnp.sum(jnp.exp(logits - row_peak[:, None]), axis=1), both)  73.5 us
    all_gather x1, waiting for transfers between devices, shards(): lax.all_gather(hidden, both, axis=0, tiled=True)  62.2 us
    all_gather x1, blocking collectives, shards(): group_queries = lax.all_gather(queries, 'keys', axis=0, tiled=True)  28.6 us
    unnamed x21, local copies, waits for them, and re-layouts  15.9 us
  transfers between devices with their start and end apart: 3, of which 2 were waited for; matrix products, arithmetic and copies ran while one was open for 4% of the time, Pallas kernels for 46%

profile of v1, /device:TPU:1, one launch (start us, length us, event | category | flops | bytes accessed | tf_op | source)
XLA Modules:
  0.0 623.1 jit_solution(9965675354229475552)
XLA Ops:
  6.5 0.7 all-gather.4.cloned.1.call-update
  7.3 2.7 multiply_reduce_fusion
  10.0 28.6 %all-gather = bf16[32,4,1024]{2,1,0:T(4,128)(2,1)} all-gather(bf16[1,4,1024]{2,1,0:T(4,128)(2,1)S(1)} %bitcast.45), channel_id=1, replica_groups=mesh['keys'=32,'vocab'=8] {'keys'}, dimensions={0}, use_global_device_ids=true | all-gather | bytes 270336 | tf_op jit(solution)/shard_map/all_gather | solution.py:97
  38.6 1.7 reshape.119
  40.3 1.1 multiply_reduce_fusion.1
  41.4 3.0 fusion.2
  44.4 1.7 reshape.88
  46.1 1.2 copy.15
  47.3 5.2 all-to-all-start
  52.7 1.9 gather_fusion
  55.3 1.0 gather_fusion.1
  56.2 1.1 reshape.86.tok_ref
  57.4 9.4 %all-to-all-done = f32[32,4,3,512]{3,1,2,0:T(4,128)S(1)} async-done(((f32[32,4,3,512]{3,1,2,0:T(4,128)}), f32[32,4,3,512]{3,1,2,0:T(4,128)S(1)}, u32[]{:S(2)}, u32[]{:S(2)}) %all-to-all-start) | async-done | bytes 786464 | tf_op jit(solution)/shard_map/all_to_all | solution.py:108
  67.0 2.1 gather_fusion.2
  69.7 1.2 copy.20
  70.9 62.2 %all-gather.4.cloned.1.call-done = bf16[256,4,4096]{2,1,0:T(4,128)(2,1)} async-done(((bf16[1,4,4096]{2,1,0:T(4,128)(2,1)}), bf16[256,4,4096]{2,1,0:T(4,128)(2,1)}) %all-gather.4.cloned.1.call-update) | async-done | bytes 8388624 | tf_op jit(solution)/shard_map/all_gather | solution.py:79
  133.1 12.5 %reshape.121 = bf16[1024,4096]{1,0:T(8,128)(2,1)} reshape(bf16[256,4,4096]{2,1,0:T(4,128)(2,1)} %all-gather.4.cloned.1.call-done) | data formatting | bytes 16777216
  145.6 8.2 %fusion.5 = (f32[1024]{0:T(1024)S(1)}, f32[1024,501]{0,1:T(8,128)S(1)}) fusion(bf16[1024,4096]{1,0:T(8,128)(2,1)} %reshape.121, bf16[4096,501]{0,1:T(8,128)(2,1)} %param.15), kind=kOutput, calls=%fused_computation.31 | convolution fusion | flops 4203204608 | bytes 14548992 | tf_op jit(solution)/shard_map/dot_general | solution.py:78
  153.8 75.1 %pmax.7 = f32[1024]{0:T(1024)S(1)} all-reduce(f32[1024]{0:T(1024)S(1)} %get-tuple-element.9), channel_id=1, replica_groups=mesh['keys'=32,'vocab'=8] {'keys','vocab'}, use_global_device_ids=true, to_apply=%region_5.6 | all-reduce | flops 1024 | bytes 8192 | tf_op jit(solution)/shard_map/pmax | solution.py:84
  229.2 73.5 %psum.7 = f32[1024]{0:T(1024)S(1)} all-reduce(f32[1024]{0:T(1024)S(1)} %exponential_reduce_fusion), channel_id=1, replica_groups=mesh['keys'=32,'vocab'=8] {'keys','vocab'}, use_global_device_ids=true, to_apply=%region_7.8 | all-reduce | flops 1024 | bytes 8192 | tf_op jit(solution)/shard_map/psum | solution.py:85
  302.7 1.0 add_convert_fusion
  303.7 1.0 copy.17
  304.8 1.1 reshape.90
  305.9 7.9 %all-to-all-start.1 = ((s16[256,4,501]{2,1,0:T(4,128)(2,1)}), s16[256,4,501]{2,1,0:T(4,128)(2,1)S(1)}, u32[]{:S(2)}, u32[]{:S(2)}) async-start(s16[256,4,501]{2,1,0:T(4,128)(2,1)} %reshape.90), calls=%async_computation.1 | async-start | bytes 2097152 | tf_op jit(solution)/shard_map/all_to_all | solution.py:93
  313.8 1.1 select_divide_fusion.w_ref
  314.9 287.3 %shard_map.82 = f32[4,1002,128]{2,1,0:T(8,128)} custom-call(s32[4,32768]{1,0:T(4,128)} %reshape.86.tok_ref, f32[4,32768]{1,0:T(4,128)} %select_divide_fusion.w_ref), custom_call_target="tpu_custom_call" | custom-call | tf_op jit(solution)/shard_map/pallas_call | solution.py:51
  602.3 2.0 compare_bitcast_fusion
  604.5 1.5 multiply_bitcast_fusion
  606.0 1.0 add_bitcast_fusion
  607.0 0.7 copy.18
  607.7 3.5 add.85
  611.2 5.0 fusion.4
  (36 shorter events, 2.2 us)
Async XLA Ops:
  6.5 48.7 %copy-start = (s32[96,512]{1,0:T(8,128)S(1)}, s32[96,512]{1,0:T(8,128)}, u32[]{:S(2)}) copy-start(s32[96,512]{1,0:T(8,128)} %param.14) | copy-start | bytes 589828
  6.5 3.5 copy-start.5
  6.5 126.6 %all-gather.4.cloned.1.call-start = ((), (), s32[]{:S(2)}) async-start(), calls=%async_computation.2 | async-start | bytes 8421376 | tf_op jit(solution)/shard_map/all_gather | solution.py:79
  7.3 34.1 %copy-start.3 = (bf16[3,512,1024]{2,1,0:T(8,128)(2,1)S(1)}, bf16[3,512,1024]{2,1,0:T(8,128)(2,1)}, u32[]{:S(2)}) copy-start(bf16[3,512,1024]{2,1,0:T(8,128)(2,1)} %param.13) | copy-start | bytes 9437188
  46.1 6.4 %copy-start.6 = (s32[4,64]{1,0:T(4,128)S(1)}, s32[4,64]{1,0:T(4,128)}, u32[]{:S(2)}) copy-start(s32[4,64]{1,0:T(4,128)} %param.10) | copy-start | bytes 3076
  46.1 6.5 %copy-start.1 = (s32[96]{0:T(128)S(1)}, s32[96]{0:T(128)}, u32[]{:S(2)}) copy-start(s32[96]{0:T(128)} %param.12) | copy-start | bytes 1156
  47.3 7.5 %copy-start.7 = (s32[4]{0:T(128)S(1)}, s32[4]{0:T(128)}, u32[]{:S(2)}) copy-start(s32[4]{0:T(128)} %param.11) | copy-start | bytes 52
  47.3 19.4 %all-to-all-start = ((f32[32,4,3,512]{3,1,2,0:T(4,128)}), f32[32,4,3,512]{3,1,2,0:T(4,128)S(1)}, u32[]{:S(2)}, u32[]{:S(2)}) async-start(f32[32,4,3,512]{3,1,2,0:T(4,128)} %copy.15), calls=%async_computation | async-start | bytes 1572864 | tf_op jit(solution)/shard_map/all_to_all | solution.py:108
  304.8 9.0 %copy-start.4 = (f32[1,4,64,512]{3,1,2,0:T(4,128)S(1)}, f32[1,4,64,512]{3,1,2,0:T(4,128)}, u32[]{:S(2)}) copy-start(f32[1,4,64,512]{3,1,2,0:T(4,128)} %copy.20) | copy-start | bytes 1572868
  305.9 300.0 %all-to-all-start.1 = ((s16[256,4,501]{2,1,0:T(4,128)(2,1)}), s16[256,4,501]{2,1,0:T(4,128)(2,1)S(1)}, u32[]{:S(2)}, u32[]{:S(2)}) async-start(s16[256,4,501]{2,1,0:T(4,128)(2,1)} %reshape.90), calls=%async_computation.1 | async-start | bytes 2097152 | tf_op jit(solution)/shard_map/all_to_all | solution.py:93
  602.3 2.2 copy-start.2
Sparse Core Ops, SparseCore 0:
  11.0 122.0 all-gather.3

commit v2 on v1

--- a/solution.py
+++ b/solution.py
@@ -10,11 +10,7 @@
 LAMBDA = 0.25
 SMOOTH = 0.1
 LANES = 128
-
-
-def code_range(vocab_size):
-    floor = LAMBDA * (SMOOTH / vocab_size) / (1.0 + SMOOTH)
-    return math.log(floor), math.log(floor + (1.0 - LAMBDA))
+CODE_DEPTH = 32.0
 
 
 def knn_kernel(tok_ref, w_ref, out_ref, *accs):
@@ -58,6 +54,11 @@
         out_specs=pl.BlockSpec((rows, lane_rows, LANES), lambda j: (0, 0, 0)),
         out_shape=jax.ShapeDtypeStruct((rows, lane_rows, LANES), jnp.float32),
         scratch_shapes=[pltpu.VMEM((lane_rows, LANES), jnp.float32) for _ in range(rows)],
+        cost_estimate=pl.CostEstimate(
+            flops=4 * rows * probes * block_len * LANES,
+            transcendentals=0,
+            bytes_accessed=rows * probes * block_len * LANES * 8,
+        ),
     )(tok, w)
     return out.reshape(rows, vocab_size)
 
@@ -80,19 +81,22 @@
         head_weight,
         preferred_element_type=jnp.float32,
     )
-    local_peak = jnp.max(logits, axis=1)
-    row_peak = lax.pmax(local_peak, both)
-    row_sum = lax.psum(jnp.sum(jnp.exp(logits - row_peak[:, None]), axis=1), both)
-    log_probs = logits - (row_peak + jnp.log(row_sum))[:, None]
-    floor = LAMBDA * (SMOOTH / vocab_size) / (1.0 + SMOOTH)
-    lo, hi = code_range(vocab_size)
-    base = jnp.log(floor + (1.0 - LAMBDA) * jnp.exp(log_probs))
-    scale = 65535.0 / (hi - lo)
-    code = (jnp.round((base - lo) * scale) - 32768.0).astype(jnp.int16)
-    sent = code.reshape(devices, rows_dev, piece_cols)
-    got = lax.all_to_all(sent, both, split_axis=0, concat_axis=0, tiled=True)
-    got = got.reshape(devices, rows_dev, piece_cols).transpose(1, 0, 2).reshape(rows_dev, vocab_size)
-    base_rows = (got.astype(jnp.float32) + 32768.0) * (1.0 / scale) + lo
+    local_peak = jnp.max(logits, axis=1, keepdims=True)
+    shifted = logits - local_peak
+    local_sum = jnp.sum(jnp.exp(shifted), axis=1, keepdims=True)
+    scale = 65535.0 / CODE_DEPTH
+    code = (jnp.round((jnp.maximum(shifted, -CODE_DEPTH) + CODE_DEPTH) * scale) - 32768.0).astype(jnp.int16)
+    got = lax.all_to_all(code.reshape(devices, rows_dev, piece_cols), both, split_axis=0, concat_axis=0, tiled=True)
+    stats = jnp.concatenate([local_peak, local_sum], axis=1).reshape(devices, rows_dev, 2)
+    got_stats = lax.all_to_all(stats, both, split_axis=0, concat_axis=0, tiled=True)
+    got = got.reshape(devices, rows_dev, piece_cols)
+    got_stats = got_stats.reshape(devices, rows_dev, 2)
+    piece_peak = got_stats[:, :, 0]
+    row_peak = jnp.max(piece_peak, axis=0)
+    row_sum = jnp.sum(got_stats[:, :, 1] * jnp.exp(piece_peak - row_peak[None, :]), axis=0)
+    offset = piece_peak - (row_peak + jnp.log(row_sum))[None, :]
+    log_probs = (got.astype(jnp.float32) + 32768.0) * (1.0 / scale) - CODE_DEPTH + offset[:, :, None]
+    log_probs = log_probs.transpose(1, 0, 2).reshape(rows_dev, vocab_size)
 
     group_queries = lax.all_gather(queries, "keys", axis=0, tiled=True)
     flat_keys = key_store.reshape(local_blocks * block_len, key_width)
@@ -114,8 +118,10 @@
     weights = raised / jnp.sum(raised, axis=(1, 2), keepdims=True)
     tokens = stored_next_tokens[slot_ids]
     knn_mass = knn_scatter(tokens, weights, vocab_size)
-    mixed = jnp.log(jnp.exp(base_rows) + (LAMBDA / (1.0 + SMOOTH)) * knn_mass)
-    return jnp.where(knn_mass > 0.0, mixed, base_rows)
+    return jnp.log(
+        LAMBDA * (knn_mass + SMOOTH / vocab_size) / (1.0 + SMOOTH)
+        + (1.0 - LAMBDA) * jnp.exp(log_probs)
+    )
 
 
 def solution(mesh):

time: 624 us -> 500 us (0.80)
  blocking collectives: 177 us -> 28.6 us
  waiting for transfers between devices: 72.4 us -> 86.6 us
  starting transfers between devices: 13.1 us -> 19.6 us
    pmax x1 -> x0, blocking collectives: 75.1 us -> none  [shards(): row_peak = lax.pmax(local_peak, both)]
    psum x1 -> x0, blocking collectives: 73.5 us -> none  [shards(): lax.psum(jnp.sum(jnp.exp(logits - row_peak[:, None]), axis=1), both)]
    all_to_all x1 -> x2, waiting for transfers between devices: 0.01 us -> 12.7 us  [the longest x1 12.7 us: shards(): lax.all_to_all(stats, both, split_axis=0, concat_axis=0, tiled=True)]
    all_to_all x1 -> x2, starting transfers between devices: 7.88 us -> 14.4 us  [the longest x1 8.46 us: shards(): lax.all_to_all(stats, both, split_axis=0, concat_axis=0, tiled=True)]
    unnamed x21 -> x17, local copies, waits for them, and re-layouts: 15.9 us -> 14.9 us
  transfers between devices with their start and end apart: 3 -> 4, of which waited for: 2 -> 3; matrix products, arithmetic and copies ran while one was open for 4% -> 5% of each run, Pallas kernels for 46% -> 58%
where the time goes in v2:
time: 500 us; the launch traced here: 499 us
  Pallas kernels  287 us (57%)
  waiting for transfers between devices  86.6 us (17%)
  local copies, waits for them, and re-layouts  32.2 us (6%)
  blocking collectives  28.6 us (6%)
  starting transfers between devices  19.6 us (4%)
  other arithmetic  17.5 us (4%)
  between operations  13.6 us (3%)
  matrix products  13.4 us (3%)
    pallas_call x1, Pallas kernels, knn_scatter(): pl.pallas_call(knn_kernel, grid=(probes,), in_specs=[pl.BlockSpec((rows,...  287 us
    all_gather x1, waiting for transfers between devices, shards(): lax.all_gather(hidden, both, axis=0, tiled=True)  63.7 us
    all_gather x1, blocking collectives, shards(): group_queries = lax.all_gather(queries, 'keys', axis=0, tiled=True)  28.6 us
    unnamed x17, local copies, waits for them, and re-layouts  14.9 us
    all_to_all x1, waiting for transfers between devices, shards(): lax.all_to_all(stats, both, split_axis=0, concat_axis=0, tiled=True)  12.7 us
    dot_general x1, matrix products, shards(): jnp.dot(lax.all_gather(hidden, both, axis=0, tiled=True), head_weight, pr...  10.3 us
  transfers between devices with their start and end apart: 4, of which 3 were waited for; matrix products, arithmetic and copies ran while one was open for 5% of the time, Pallas kernels for 58%

profile of v2, /device:TPU:1, one launch (start us, length us, event | category | flops | bytes accessed | tf_op | source)
XLA Modules:
  0.0 498.8 jit_solution(5959556033412237937)
XLA Ops:
  6.5 0.7 all-gather.4.cloned.1.call-update
  7.3 2.7 multiply_reduce_fusion
  10.0 28.6 %all-gather = bf16[32,4,1024]{2,1,0:T(4,128)(2,1)} all-gather(bf16[1,4,1024]{2,1,0:T(4,128)(2,1)S(1)} %bitcast.49), channel_id=1, replica_groups=mesh['keys'=32,'vocab'=8] {'keys'}, dimensions={0}, use_global_device_ids=true | all-gather | bytes 270336 | tf_op jit(solution)/shard_map/all_gather | solution.py:101
  38.6 1.7 reshape.133
  40.3 1.1 multiply_reduce_fusion.1
  41.4 3.0 fusion.2
  44.4 1.7 reshape.102
  46.1 1.2 copy.23
  47.3 5.2 %all-to-all-start = ((f32[32,4,3,512]{3,1,2,0:T(4,128)}), f32[32,4,3,512]{3,1,2,0:T(4,128)S(1)}, u32[]{:S(2)}, u32[]{:S(2)}) async-start(f32[32,4,3,512]{3,1,2,0:T(4,128)} %copy.23), calls=%async_computation | async-start | bytes 1572864 | tf_op jit(solution)/shard_map/all_to_all | solution.py:112
  52.7 1.9 gather_fusion
  55.3 1.0 gather_fusion.1
  56.2 1.1 reshape.100.tok_ref
  57.4 9.4 %all-to-all-done = f32[32,4,3,512]{3,1,2,0:T(4,128)S(1)} async-done(((f32[32,4,3,512]{3,1,2,0:T(4,128)}), f32[32,4,3,512]{3,1,2,0:T(4,128)S(1)}, u32[]{:S(2)}, u32[]{:S(2)}) %all-to-all-start) | async-done | bytes 786464 | tf_op jit(solution)/shard_map/all_to_all | solution.py:112
  67.0 2.1 gather_fusion.2
  69.4 63.7 %all-gather.4.cloned.1.call-done = bf16[256,4,4096]{2,1,0:T(4,128)(2,1)} async-done(((bf16[1,4,4096]{2,1,0:T(4,128)(2,1)}), bf16[256,4,4096]{2,1,0:T(4,128)(2,1)}) %all-gather.4.cloned.1.call-update) | async-done | bytes 8388624 | tf_op jit(solution)/shard_map/all_gather | solution.py:80
  133.1 12.5 %reshape.135 = bf16[1024,4096]{1,0:T(8,128)(2,1)} reshape(bf16[256,4,4096]{2,1,0:T(4,128)(2,1)} %all-gather.4.cloned.1.call-done) | data formatting | bytes 16777216
  145.6 10.3 %fusion.5 = (f32[1024]{0:T(1024)S(1)}, f32[1024,501]{0,1:T(8,128)}) fusion(bf16[1024,4096]{1,0:T(8,128)(2,1)} %reshape.135, bf16[4096,501]{0,1:T(8,128)(2,1)} %param.15), kind=kOutput, calls=%fused_computation.33 | convolution fusion | flops 4203204608 | bytes 14548992 | tf_op jit(solution)/shard_map/dot_general | solution.py:79
  156.1 2.5 exponential_reduce_fusion
  158.7 0.9 copy.26
  159.6 8.5 %all-to-all-start.2 = ((f32[256,4,2]{1,2,0:T(2,128)}), f32[256,4,2]{1,2,0:T(2,128)S(1)}, u32[]{:S(2)}, u32[]{:S(2)}) async-start(f32[256,4,2]{1,2,0:T(2,128)} %copy.26), calls=%async_computation.2 | async-start | bytes 524288 | tf_op jit(solution)/shard_map/all_to_all | solution.py:91
  168.4 0.3 copy.31
  168.8 1.0 copy.25
  169.8 1.1 reshape.104
  171.0 12.7 %all-to-all-done.2 = f32[256,4,2]{1,2,0:T(2,128)S(1)} async-done(((f32[256,4,2]{1,2,0:T(2,128)}), f32[256,4,2]{1,2,0:T(2,128)S(1)}, u32[]{:S(2)}, u32[]{:S(2)}) %all-to-all-start.2) | async-done | bytes 8224 | tf_op jit(solution)/shard_map/all_to_all | solution.py:91
  183.7 6.0 %all-to-all-start.1 = ((s16[256,4,501]{2,1,0:T(4,128)(2,1)}), s16[256,4,501]{2,1,0:T(4,128)(2,1)S(1)}, u32[]{:S(2)}, u32[]{:S(2)}) async-start(s16[256,4,501]{2,1,0:T(4,128)(2,1)} %reshape.104), calls=%async_computation.1 | async-start | bytes 2097152 | tf_op jit(solution)/shard_map/all_to_all | solution.py:89
  189.7 1.1 select_divide_fusion.w_ref
  190.8 287.3 %shard_map.82 = f32[4,1002,128]{2,1,0:T(8,128)} custom-call(s32[4,32768]{1,0:T(4,128)} %reshape.100.tok_ref, f32[4,32768]{1,0:T(4,128)} %select_divide_fusion.w_ref), custom_call_target="tpu_custom_call" | custom-call | flops 67108864 | bytes 134217728 | tf_op jit(solution)/shard_map/pallas_call | solution.py:47
  478.1 3.2 multiply_bitcast_fusion.1
  481.7 1.5 multiply_bitcast_fusion
  483.2 0.7 copy.28
  483.9 3.5 mul.53
  487.4 4.6 fusion.3
  (38 shorter events, 2.3 us)
Async XLA Ops:
  6.5 48.7 %copy-start = (s32[96,512]{1,0:T(8,128)S(1)}, s32[96,512]{1,0:T(8,128)}, u32[]{:S(2)}) copy-start(s32[96,512]{1,0:T(8,128)} %param.14) | copy-start | bytes 589828
  6.5 3.5 copy-start.3
  6.5 126.6 %all-gather.4.cloned.1.call-start = ((), (), s32[]{:S(2)}) async-start(), calls=%async_computation.3 | async-start | bytes 8421376 | tf_op jit(solution)/shard_map/all_gather | solution.py:80
  7.3 34.1 %copy-start.2 = (bf16[3,512,1024]{2,1,0:T(8,128)(2,1)S(1)}, bf16[3,512,1024]{2,1,0:T(8,128)(2,1)}, u32[]{:S(2)}) copy-start(bf16[3,512,1024]{2,1,0:T(8,128)(2,1)} %param.13) | copy-start | bytes 9437188
  46.1 6.4 %copy-start.4 = (s32[4,64]{1,0:T(4,128)S(1)}, s32[4,64]{1,0:T(4,128)}, u32[]{:S(2)}) copy-start(s32[4,64]{1,0:T(4,128)} %param.10) | copy-start | bytes 3076
  46.1 6.5 %copy-start.1 = (s32[96]{0:T(128)S(1)}, s32[96]{0:T(128)}, u32[]{:S(2)}) copy-start(s32[96]{0:T(128)} %param.12) | copy-start | bytes 1156
  47.3 7.5 %copy-start.5 = (s32[4]{0:T(128)S(1)}, s32[4]{0:T(128)}, u32[]{:S(2)}) copy-start(s32[4]{0:T(128)} %param.11) | copy-start | bytes 52
  47.3 19.4 %all-to-all-start = ((f32[32,4,3,512]{3,1,2,0:T(4,128)}), f32[32,4,3,512]{3,1,2,0:T(4,128)S(1)}, u32[]{:S(2)}, u32[]{:S(2)}) async-start(f32[32,4,3,512]{3,1,2,0:T(4,128)} %copy.23), calls=%async_computation | async-start | bytes 1572864 | tf_op jit(solution)/shard_map/all_to_all | solution.py:112
  159.6 24.0 %all-to-all-start.2 = ((f32[256,4,2]{1,2,0:T(2,128)}), f32[256,4,2]{1,2,0:T(2,128)S(1)}, u32[]{:S(2)}, u32[]{:S(2)}) async-start(f32[256,4,2]{1,2,0:T(2,128)} %copy.26), calls=%async_computation.2 | async-start | bytes 524288 | tf_op jit(solution)/shard_map/all_to_all | solution.py:91
  183.7 298.0 %all-to-all-start.1 = ((s16[256,4,501]{2,1,0:T(4,128)(2,1)}), s16[256,4,501]{2,1,0:T(4,128)(2,1)S(1)}, u32[]{:S(2)}, u32[]{:S(2)}) async-start(s16[256,4,501]{2,1,0:T(4,128)(2,1)} %reshape.104), calls=%async_computation.1 | async-start | bytes 2097152 | tf_op jit(solution)/shard_map/all_to_all | solution.py:89
Sparse Core Ops, SparseCore 0:
  11.0 122.0 all-gather.3

commit v3 on v2

--- a/solution.py
+++ b/solution.py
@@ -13,13 +13,13 @@
 CODE_DEPTH = 32.0
 
 
-def knn_kernel(tok_ref, w_ref, out_ref, *accs):
+def knn_kernel(tok_ref, w_ref, init_ref, out_ref, *accs):
     step = pl.program_id(0)
 
     @pl.when(step == 0)
     def _():
-        for acc in accs:
-            acc[...] = jnp.zeros_like(acc)
+        for r, acc in enumerate(accs):
+            acc[...] = init_ref[r]
 
     lane = lax.broadcasted_iota(jnp.int32, (1, LANES), 1)
 
@@ -39,17 +39,18 @@
             out_ref[r] = acc[...]
 
 
-def knn_scatter(tokens, weights, vocab_size):
+def knn_scatter(tokens, weights, init):
     rows, probes, block_len = tokens.shape
     tok = tokens.reshape(rows, probes * block_len)
     w = weights.reshape(rows, probes * block_len)
-    lane_rows = vocab_size // LANES
+    lane_rows = init.shape[1]
     out = pl.pallas_call(
         knn_kernel,
         grid=(probes,),
         in_specs=[
             pl.BlockSpec((rows, block_len), lambda j: (0, j), memory_space=pltpu.SMEM),
             pl.BlockSpec((rows, block_len), lambda j: (0, j), memory_space=pltpu.SMEM),
+            pl.BlockSpec((rows, lane_rows, LANES), lambda j: (0, 0, 0)),
         ],
         out_specs=pl.BlockSpec((rows, lane_rows, LANES), lambda j: (0, 0, 0)),
         out_shape=jax.ShapeDtypeStruct((rows, lane_rows, LANES), jnp.float32),
@@ -57,10 +58,11 @@
         cost_estimate=pl.CostEstimate(
             flops=4 * rows * probes * block_len * LANES,
             transcendentals=0,
-            bytes_accessed=rows * probes * block_len * LANES * 8,
+            bytes_accessed=rows * probes * block_len * LANES * 8 + 8 * rows * lane_rows * LANES,
         ),
-    )(tok, w)
-    return out.reshape(rows, vocab_size)
+        input_output_aliases={2: 0},
+    )(tok, w, init)
+    return out
 
 
 def shards(hidden, queries, probes, counts, block_slot, key_store, stored_next_tokens, head_weight):
@@ -75,28 +77,6 @@
     probe_cap = probes.shape[1]
     vocab_size = devices * piece_cols
     both = ("keys", "vocab")
-
-    logits = jnp.dot(
-        lax.all_gather(hidden, both, axis=0, tiled=True),
-        head_weight,
-        preferred_element_type=jnp.float32,
-    )
-    local_peak = jnp.max(logits, axis=1, keepdims=True)
-    shifted = logits - local_peak
-    local_sum = jnp.sum(jnp.exp(shifted), axis=1, keepdims=True)
-    scale = 65535.0 / CODE_DEPTH
-    code = (jnp.round((jnp.maximum(shifted, -CODE_DEPTH) + CODE_DEPTH) * scale) - 32768.0).astype(jnp.int16)
-    got = lax.all_to_all(code.reshape(devices, rows_dev, piece_cols), both, split_axis=0, concat_axis=0, tiled=True)
-    stats = jnp.concatenate([local_peak, local_sum], axis=1).reshape(devices, rows_dev, 2)
-    got_stats = lax.all_to_all(stats, both, split_axis=0, concat_axis=0, tiled=True)
-    got = got.reshape(devices, rows_dev, piece_cols)
-    got_stats = got_stats.reshape(devices, rows_dev, 2)
-    piece_peak = got_stats[:, :, 0]
-    row_peak = jnp.max(piece_peak, axis=0)
-    row_sum = jnp.sum(got_stats[:, :, 1] * jnp.exp(piece_peak - row_peak[None, :]), axis=0)
-    offset = piece_peak - (row_peak + jnp.log(row_sum))[None, :]
-    log_probs = (got.astype(jnp.float32) + 32768.0) * (1.0 / scale) - CODE_DEPTH + offset[:, :, None]
-    log_probs = log_probs.transpose(1, 0, 2).reshape(rows_dev, vocab_size)
 
     group_queries = lax.all_gather(queries, "keys", axis=0, tiled=True)
     flat_keys = key_store.reshape(local_blocks * block_len, key_width)
@@ -117,7 +97,31 @@
     raised = jnp.where(live_mask, jnp.exp(chosen - best_score), 0.0)
     weights = raised / jnp.sum(raised, axis=(1, 2), keepdims=True)
     tokens = stored_next_tokens[slot_ids]
-    knn_mass = knn_scatter(tokens, weights, vocab_size)
+    half = probe_cap // 2
+    zeros = jnp.zeros((rows_dev, vocab_size // LANES, LANES), jnp.float32)
+    knn_first = knn_scatter(tokens[:, :half], weights[:, :half], zeros)
+    gathered = lax.all_gather(hidden, both, axis=0, tiled=False)
+    gathered, knn_first = lax.optimization_barrier((gathered, knn_first))
+    logits = jnp.einsum("dri,ic->drc", gathered, head_weight, preferred_element_type=jnp.float32)
+    local_peak = jnp.max(logits, axis=2, keepdims=True)
+    shifted = logits - local_peak
+    local_sum = jnp.sum(jnp.exp(shifted), axis=2, keepdims=True)
+    scale = 65535.0 / CODE_DEPTH
+    code = (jnp.round((jnp.maximum(shifted, -CODE_DEPTH) + CODE_DEPTH) * scale) - 32768.0).astype(jnp.int16)
+    stats = jnp.concatenate([local_peak, local_sum], axis=2)
+    code, stats, knn_first = lax.optimization_barrier((code, stats, knn_first))
+    got = lax.all_to_all(code, both, split_axis=0, concat_axis=0, tiled=True)
+    got_stats = lax.all_to_all(stats, both, split_axis=0, concat_axis=0, tiled=True)
+    knn_mass = knn_scatter(tokens[:, half:], weights[:, half:], knn_first).reshape(rows_dev, vocab_size)
+    got = got.reshape(devices, rows_dev, piece_cols)
+    got_stats = got_stats.reshape(devices, rows_dev, 2)
+    piece_peak = got_stats[:, :, 0]
+    row_peak = jnp.max(piece_peak, axis=0)
+    row_sum = jnp.sum(got_stats[:, :, 1] * jnp.exp(piece_peak - row_peak[None, :]), axis=0)
+    offset = piece_peak - (row_peak + jnp.log(row_sum))[None, :]
+    log_probs = (got.astype(jnp.float32) + 32768.0) * (1.0 / scale) - CODE_DEPTH + offset[:, :, None]
+    log_probs = log_probs.transpose(1, 0, 2).reshape(rows_dev, vocab_size)
+
     return jnp.log(
         LAMBDA * (knn_mass + SMOOTH / vocab_size) / (1.0 + SMOOTH)
         + (1.0 - LAMBDA) * jnp.exp(log_probs)

time: 500 us -> 440 us (0.88)
  waiting for transfers between devices: 86.6 us -> 24.2 us
  Pallas kernels: 287 us -> 298 us
  local copies, waits for them, and re-layouts: 32.2 us -> 25 us
    all_gather x1, waiting for transfers between devices: 63.7 us -> 0.01 us  [shards(): gathered = lax.all_gather(hidden, both, axis=0, tiled=False)]
    pallas_call x1 -> x2, Pallas kernels: 287 us -> 298 us  [knn_scatter(): pl.pallas_call(knn_kernel, grid=(probes,), in_specs=[pl.BlockSpec((rows,...]
    unnamed x17, local copies, waits for them, and re-layouts: 14.9 us -> 5.31 us
  transfers between devices with their start and end apart: 4 -> 4, of which waited for: 3 -> 2; matrix products, arithmetic and copies ran while one was open for 5% -> 6% of each run, Pallas kernels for 58% -> 68%
where the time goes in v3:
time: 440 us
  Pallas kernels  298 us (68%)
  blocking collectives  29.3 us (7%)
  local copies, waits for them, and re-layouts  25 us (6%)
  waiting for transfers between devices  24.2 us (6%)
  starting transfers between devices  21.2 us (5%)
  other arithmetic  15.4 us (4%)
  between operations  13.6 us (3%)
  matrix products  13.2 us (3%)
    pallas_call x2, Pallas kernels, knn_scatter(): pl.pallas_call(knn_kernel, grid=(probes,), in_specs=[pl.BlockSpec((rows,...  298 us
    all_gather x1, blocking collectives, shards(): group_queries = lax.all_gather(queries, 'keys', axis=0, tiled=True)  29.3 us
    all_to_all x1, waiting for transfers between devices, shards(): lax.all_to_all(stats, both, split_axis=0, concat_axis=0, tiled=True)  13.6 us
    all_to_all x1, starting transfers between devices, shards(): lax.all_to_all(stats, both, split_axis=0, concat_axis=0, tiled=True)  10.9 us
    dot_general x1, matrix products, shards(): jnp.einsum('dri,ic->drc', gathered, head_weight, preferred_element_type=j...  10.1 us
    all_to_all x1, waiting for transfers between devices, shards(): lax.all_to_all(outgoing, 'keys', split_axis=0, concat_axis=2, tiled=True)  9.9 us
  transfers between devices with their start and end apart: 4, of which 2 were waited for; matrix products, arithmetic and copies ran while one was open for 6% of the time, Pallas kernels for 68%

profile of v3, /device:TPU:1, one launch (start us, length us, event | category | flops | bytes accessed | tf_op | source)
XLA Modules:
  0.0 439.7 jit_solution(4314936408619340679)
XLA Ops:
  7.3 29.3 %all-gather.1 = bf16[32,4,1024]{2,1,0:T(4,128)(2,1)} all-gather(bf16[1,4,1024]{2,1,0:T(4,128)(2,1)} %bitcast.66), channel_id=1, replica_groups=mesh['keys'=32,'vocab'=8] {'keys'}, dimensions={0}, use_global_device_ids=true | all-gather | bytes 270336 | tf_op jit(solution)/shard_map/all_gather | solution.py:81
  36.6 1.7 reshape.130
  38.3 2.6 multiply_reduce_fusion
  40.9 1.1 multiply_reduce_fusion.1
  42.0 3.0 fusion.5
  45.0 1.7 reshape.97
  46.7 1.2 copy.26
  47.9 4.6 %all-to-all-start = ((f32[32,4,3,512]{3,1,2,0:T(4,128)}), f32[32,4,3,512]{3,1,2,0:T(4,128)S(1)}, u32[]{:S(2)}, u32[]{:S(2)}) async-start(f32[32,4,3,512]{3,1,2,0:T(4,128)} %copy.26), calls=%async_computation | async-start | bytes 1572864 | tf_op jit(solution)/shard_map/all_to_all | solution.py:92
  52.6 1.9 gather_fusion
  54.9 1.0 gather_fusion.1
  55.9 0.9 copy.38
  56.9 9.9 %all-to-all-done = f32[32,4,3,512]{3,1,2,0:T(4,128)S(1)} async-done(((f32[32,4,3,512]{3,1,2,0:T(4,128)}), f32[32,4,3,512]{3,1,2,0:T(4,128)S(1)}, u32[]{:S(2)}, u32[]{:S(2)}) %all-to-all-start) | async-done | bytes 786464 | tf_op jit(solution)/shard_map/all_to_all | solution.py:92
  67.0 2.1 gather_fusion.2
  69.9 0.9 copy.39
  70.8 1.5 broadcast_in_dim.56.init_ref
  72.3 148.9 %shard_map.82.init_ref = f32[4,1002,128]{2,1,0:T(8,128)} custom-call(s32[4,16384]{1,0:T(4,128)} %bitcast.58, f32[4,16384]{1,0:T(4,128)} %bitcast.60, f32[4,1002,128]{2,1,0:T(8,128)} %broadcast_in_dim.56.init_ref), custom_call_target="tpu_custom_call", output_to_operand_aliasing={{}: (2, {})} | custom-call | flops 33554432 | bytes 71213056 | tf_op jit(solution)/shard_map/pallas_call | solution.py:47
  221.2 10.1 %fusion.10 = (f32[256,4]{0,1:T(4,128)S(1)}, f32[256,4,501]{0,2,1:T(8,128)S(1)}) fusion(bf16[4096,501]{0,1:T(8,128)(2,1)} %param.15, bf16[256,4,4096]{2,1,0:T(4,128)(2,1)} %all-gather.5.cloned.1.call-done), kind=kOutput, calls=%fused_computation.39 | convolution fusion | flops 4203204608 | bytes 14548992 | tf_op jit(solution)/shard_map/dri,ic->drc/dot_general | solution.py:105
  231.3 0.9 exponential_reduce_fusion
  232.3 0.8 copy.31
  233.1 10.9 %all-to-all-start.2 = ((f32[256,4,2]{1,2,0:T(2,128)}), f32[256,4,2]{1,2,0:T(2,128)S(1)}, u32[]{:S(2)}, u32[]{:S(2)}) async-start(f32[256,4,2]{1,2,0:T(2,128)} %copy.31), calls=%async_computation.2 | async-start | bytes 524288 | tf_op jit(solution)/shard_map/all_to_all | solution.py:114
  244.0 2.0 copy.29
  246.0 13.6 %all-to-all-done.2 = f32[256,4,2]{1,2,0:T(2,128)S(1)} async-done(((f32[256,4,2]{1,2,0:T(2,128)}), f32[256,4,2]{1,2,0:T(2,128)S(1)}, u32[]{:S(2)}, u32[]{:S(2)}) %all-to-all-start.2) | async-done | bytes 8224 | tf_op jit(solution)/shard_map/all_to_all | solution.py:114
  259.6 5.8 %all-to-all-start.1 = ((s16[256,4,501]{2,1,0:T(4,128)(2,1)}), s16[256,4,501]{2,1,0:T(4,128)(2,1)S(1)}, u32[]{:S(2)}, u32[]{:S(2)}) async-start(s16[256,4,501]{2,1,0:T(4,128)(2,1)} %copy.29), calls=%async_computation.1 | async-start | bytes 2097152 | tf_op jit(solution)/shard_map/all_to_all | solution.py:113
  265.3 0.9 copy.36
  266.2 0.9 copy.37
  267.1 148.9 %shard_map.83 = f32[4,1002,128]{2,1,0:T(8,128)} custom-call(s32[4,16384]{1,0:T(4,128)} %bitcast.59, f32[4,16384]{1,0:T(4,128)} %bitcast.61, f32[4,1002,128]{2,1,0:T(8,128)} %shard_map.82.init_ref), custom_call_target="tpu_custom_call", output_to_operand_aliasing={{}: (2, {})} | custom-call | flops 33554432 | bytes 71213056 | tf_op jit(solution)/shard_map/pallas_call | solution.py:47
  416.0 3.2 multiply_bitcast_fusion.1
  419.6 1.2 copy.30
  420.8 2.0 multiply_bitcast_fusion
  422.8 1.9 copy.34
  424.7 3.5 mul.53
  428.2 4.6 %fusion.6 = f32[4,128256]{1,0:T(4,128)} fusion(f32[4,128256]{1,0:T(4,128)} %mul.53, f32[1,4,1002,128]{3,2,1,0:T(8,128)} %multiply_bitcast_fusion.1), kind=kLoop, calls=%fused_computation.16 | loop fusion | flops 513024 | bytes 6156288 | tf_op jit(solution)/shard_map/log | solution.py:125
  (38 shorter events, 2.7 us)
Async XLA Ops:
  6.5 48.3 %copy-start = (s32[96,512]{1,0:T(8,128)S(1)}, s32[96,512]{1,0:T(8,128)}, u32[]{:S(2)}) copy-start(s32[96,512]{1,0:T(8,128)} %param.14) | copy-start | bytes 589828
  6.5 214.6 %all-gather.5.cloned.1.call-start = ((), (), s32[]{:S(2)}) async-start(), calls=%async_computation.3 | async-start | bytes 8421376 | tf_op jit(solution)/shard_map/all_gather | solution.py:103
  7.3 34.7 %copy-start.2 = (bf16[3,512,1024]{2,1,0:T(8,128)(2,1)S(1)}, bf16[3,512,1024]{2,1,0:T(8,128)(2,1)}, u32[]{:S(2)}) copy-start(bf16[3,512,1024]{2,1,0:T(8,128)(2,1)} %param.13) | copy-start | bytes 9437188
  46.7 5.9 %copy-start.3 = (s32[4,64]{1,0:T(4,128)S(1)}, s32[4,64]{1,0:T(4,128)}, u32[]{:S(2)}) copy-start(s32[4,64]{1,0:T(4,128)} %param.10) | copy-start | bytes 3076
  46.7 6.0 %copy-start.1 = (s32[96]{0:T(128)S(1)}, s32[96]{0:T(128)}, u32[]{:S(2)}) copy-start(s32[96]{0:T(128)} %param.12) | copy-start | bytes 1156
  47.9 18.9 %all-to-all-start = ((f32[32,4,3,512]{3,1,2,0:T(4,128)}), f32[32,4,3,512]{3,1,2,0:T(4,128)S(1)}, u32[]{:S(2)}, u32[]{:S(2)}) async-start(f32[32,4,3,512]{3,1,2,0:T(4,128)} %copy.26), calls=%async_computation | async-start | bytes 1572864 | tf_op jit(solution)/shard_map/all_to_all | solution.py:92
  54.9 1.9 copy-start.4
  233.1 26.5 %all-to-all-start.2 = ((f32[256,4,2]{1,2,0:T(2,128)}), f32[256,4,2]{1,2,0:T(2,128)S(1)}, u32[]{:S(2)}, u32[]{:S(2)}) async-start(f32[256,4,2]{1,2,0:T(2,128)} %copy.31), calls=%async_computation.2 | async-start | bytes 524288 | tf_op jit(solution)/shard_map/all_to_all | solution.py:114
  259.6 160.0 %all-to-all-start.1 = ((s16[256,4,501]{2,1,0:T(4,128)(2,1)}), s16[256,4,501]{2,1,0:T(4,128)(2,1)S(1)}, u32[]{:S(2)}, u32[]{:S(2)}) async-start(s16[256,4,501]{2,1,0:T(4,128)(2,1)} %copy.29), calls=%async_computation.1 | async-start | bytes 2097152 | tf_op jit(solution)/shard_map/all_to_all | solution.py:113
Sparse Core Ops, SparseCore 0:
  11.0 122.0 all-gather.4

commit v4 on v3

--- a/solution.py
+++ b/solution.py
@@ -10,7 +10,6 @@
 LAMBDA = 0.25
 SMOOTH = 0.1
 LANES = 128
-CODE_DEPTH = 32.0
 
 
 def knn_kernel(tok_ref, w_ref, init_ref, out_ref, *accs):
@@ -106,20 +105,16 @@
     local_peak = jnp.max(logits, axis=2, keepdims=True)
     shifted = logits - local_peak
     local_sum = jnp.sum(jnp.exp(shifted), axis=2, keepdims=True)
-    scale = 65535.0 / CODE_DEPTH
-    code = (jnp.round((jnp.maximum(shifted, -CODE_DEPTH) + CODE_DEPTH) * scale) - 32768.0).astype(jnp.int16)
-    stats = jnp.concatenate([local_peak, local_sum], axis=2)
-    code, stats, knn_first = lax.optimization_barrier((code, stats, knn_first))
-    got = lax.all_to_all(code, both, split_axis=0, concat_axis=0, tiled=True)
-    got_stats = lax.all_to_all(stats, both, split_axis=0, concat_axis=0, tiled=True)
+    payload = jnp.concatenate([shifted, local_peak, local_sum], axis=2)
+    payload, knn_first = lax.optimization_barrier((payload, knn_first))
+    got = lax.all_to_all(payload, both, split_axis=0, concat_axis=0, tiled=True)
     knn_mass = knn_scatter(tokens[:, half:], weights[:, half:], knn_first).reshape(rows_dev, vocab_size)
-    got = got.reshape(devices, rows_dev, piece_cols)
-    got_stats = got_stats.reshape(devices, rows_dev, 2)
-    piece_peak = got_stats[:, :, 0]
+    got = got.reshape(devices, rows_dev, piece_cols + 2)
+    piece_peak = got[:, :, piece_cols]
     row_peak = jnp.max(piece_peak, axis=0)
-    row_sum = jnp.sum(got_stats[:, :, 1] * jnp.exp(piece_peak - row_peak[None, :]), axis=0)
+    row_sum = jnp.sum(got[:, :, piece_cols + 1] * jnp.exp(piece_peak - row_peak[None, :]), axis=0)
     offset = piece_peak - (row_peak + jnp.log(row_sum))[None, :]
-    log_probs = (got.astype(jnp.float32) + 32768.0) * (1.0 / scale) - CODE_DEPTH + offset[:, :, None]
+    log_probs = got[:, :, :piece_cols] + offset[:, :, None]
     log_probs = log_probs.transpose(1, 0, 2).reshape(rows_dev, vocab_size)
 
     return jnp.log(

time: 440 us -> 417 us (0.948)
  waiting for transfers between devices: 24.2 us -> 10.6 us
  starting transfers between devices: 21.2 us -> 15.5 us
    all_to_all x2 -> x1, waiting for transfers between devices: 13.6 us -> 0.01 us  [shards(): got = lax.all_to_all(payload, both, split_axis=0, concat_axis=0, tiled=True)]
    all_to_all x2 -> x1, starting transfers between devices: 16.6 us -> 10.9 us  [shards(): got = lax.all_to_all(payload, both, split_axis=0, concat_axis=0, tiled=True)]
  transfers between devices with their start and end apart: 4 -> 3, of which waited for: 2 -> 1; matrix products, arithmetic and copies ran while one was open for 6% -> 6% of each run, Pallas kernels for 68% -> 72%
where the time goes in v4:
time: 417 us; the launch traced here: 416 us
  Pallas kernels  298 us (71%)
  blocking collectives  29.3 us (7%)
  local copies, waits for them, and re-layouts  22.2 us (5%)
  starting transfers between devices  15.5 us (4%)
  other arithmetic  14.4 us (3%)
  between operations  13.6 us (3%)
  matrix products  13.2 us (3%)
  waiting for transfers between devices  10.6 us (3%)
    pallas_call x2, Pallas kernels, knn_scatter(): pl.pallas_call(knn_kernel, grid=(probes,), in_specs=[pl.BlockSpec((rows,...  298 us
    all_gather x1, blocking collectives, shards(): group_queries = lax.all_gather(queries, 'keys', axis=0, tiled=True)  29.3 us
    all_to_all x1, starting transfers between devices, shards(): got = lax.all_to_all(payload, both, split_axis=0, concat_axis=0, tiled=True)  10.9 us
    dot_general x1, matrix products, shards(): jnp.einsum('dri,ic->drc', gathered, head_weight, preferred_element_type=j...  10.1 us
    all_to_all x1, waiting for transfers between devices, shards(): lax.all_to_all(outgoing, 'keys', split_axis=0, concat_axis=2, tiled=True)  9.9 us
  transfers between devices with their start and end apart: 3, of which 1 were waited for; matrix products, arithmetic and copies ran while one was open for 6% of the time, Pallas kernels for 72%

profile of v4, /device:TPU:1, one launch (start us, length us, event | category | flops | bytes accessed | tf_op | source)
XLA Modules:
  0.0 416.4 jit_solution(4829906794846416098)
XLA Ops:
  6.5 0.7 all-gather.5.cloned.1.call-update
  7.3 29.3 %all-gather.1 = bf16[32,4,1024]{2,1,0:T(4,128)(2,1)} all-gather(bf16[1,4,1024]{2,1,0:T(4,128)(2,1)} %bitcast.68), channel_id=1, replica_groups=mesh['keys'=32,'vocab'=8] {'keys'}, dimensions={0}, use_global_device_ids=true | all-gather | bytes 270336 | tf_op jit(solution)/shard_map/all_gather | solution.py:80
  36.6 1.7 reshape.130
  38.3 2.6 multiply_reduce_fusion
  40.9 1.1 multiply_reduce_fusion.1
  42.0 3.0 fusion.5
  45.0 1.7 reshape.97
  46.7 1.2 copy.25
  47.9 4.6 %all-to-all-start = ((f32[32,4,3,512]{3,1,2,0:T(4,128)}), f32[32,4,3,512]{3,1,2,0:T(4,128)S(1)}, u32[]{:S(2)}, u32[]{:S(2)}) async-start(f32[32,4,3,512]{3,1,2,0:T(4,128)} %copy.25), calls=%async_computation | async-start | bytes 1572864 | tf_op jit(solution)/shard_map/all_to_all | solution.py:91
  52.6 1.9 gather_fusion
  54.9 1.0 gather_fusion.1
  55.9 0.9 copy.37
  56.9 9.9 %all-to-all-done = f32[32,4,3,512]{3,1,2,0:T(4,128)S(1)} async-done(((f32[32,4,3,512]{3,1,2,0:T(4,128)}), f32[32,4,3,512]{3,1,2,0:T(4,128)S(1)}, u32[]{:S(2)}, u32[]{:S(2)}) %all-to-all-start) | async-done | bytes 786464 | tf_op jit(solution)/shard_map/all_to_all | solution.py:91
  66.8 0.3 copy.26
  67.0 2.1 gather_fusion.2
  69.4 0.3 fusion.11
  69.9 0.9 copy.38
  70.8 1.5 broadcast_in_dim.56.init_ref
  72.3 148.9 %shard_map.82.init_ref = f32[4,1002,128]{2,1,0:T(8,128)} custom-call(s32[4,16384]{1,0:T(4,128)} %bitcast.63, f32[4,16384]{1,0:T(4,128)} %bitcast.65, f32[4,1002,128]{2,1,0:T(8,128)} %broadcast_in_dim.56.init_ref), custom_call_target="tpu_custom_call", output_to_operand_aliasing={{}: (2, {})} | custom-call | flops 33554432 | bytes 71213056 | tf_op jit(solution)/shard_map/pallas_call | solution.py:46
  221.2 10.1 %fusion.16 = (f32[256,4]{0,1:T(4,128)S(1)}, f32[256,4,501]{0,2,1:T(8,128)S(1)}) fusion(bf16[4096,501]{0,1:T(8,128)(2,1)} %param.15, bf16[256,4,4096]{2,1,0:T(4,128)(2,1)} %all-gather.5.cloned.1.call-done), kind=kOutput, calls=%fused_computation.46 | convolution fusion | flops 4203204608 | bytes 14548992 | tf_op jit(solution)/shard_map/dri,ic->drc/dot_general | solution.py:104
  231.3 0.3 exponential_reduce_fusion
  231.8 2.0 copy.28
  233.8 10.9 %all-to-all-start.1 = ((f32[256,4,503]{2,1,0:T(4,128)}), f32[256,4,503]{2,1,0:T(4,128)S(1)}, u32[]{:S(2)}, u32[]{:S(2)}) async-start(f32[256,4,503]{2,1,0:T(4,128)} %copy.28), calls=%async_computation.1 | async-start | bytes 4194304 | tf_op jit(solution)/shard_map/all_to_all | solution.py:110
  244.7 0.9 copy.35
  245.5 0.9 copy.36
  246.4 148.9 %shard_map.83 = f32[4,1002,128]{2,1,0:T(8,128)} custom-call(s32[4,16384]{1,0:T(4,128)} %bitcast.64, f32[4,16384]{1,0:T(4,128)} %bitcast.66, f32[4,1002,128]{2,1,0:T(8,128)} %shard_map.82.init_ref), custom_call_target="tpu_custom_call", output_to_operand_aliasing={{}: (2, {})} | custom-call | flops 33554432 | bytes 71213056 | tf_op jit(solution)/shard_map/pallas_call | solution.py:46
  395.3 3.1 multiply_bitcast_fusion
  398.5 0.7 fusion.15
  400.0 0.8 fusion.8
  400.8 0.7 copy.32
  401.5 3.5 mul.37
  405.0 4.6 %fusion.9 = f32[4,128256]{1,0:T(4,128)} fusion(f32[4,128256]{1,0:T(4,128)} %mul.37, f32[1,4,1002,128]{3,2,1,0:T(8,128)} %multiply_bitcast_fusion), kind=kLoop, calls=%fused_computation.19 | loop fusion | flops 513024 | bytes 6156288 | tf_op jit(solution)/shard_map/log | solution.py:120
  (37 shorter events, 2.0 us)
Async XLA Ops:
  6.5 48.3 %copy-start = (s32[96,512]{1,0:T(8,128)S(1)}, s32[96,512]{1,0:T(8,128)}, u32[]{:S(2)}) copy-start(s32[96,512]{1,0:T(8,128)} %param.14) | copy-start | bytes 589828
  6.5 214.6 %all-gather.5.cloned.1.call-start = ((), (), s32[]{:S(2)}) async-start(), calls=%async_computation.2 | async-start | bytes 8421376 | tf_op jit(solution)/shard_map/all_gather | solution.py:102
  7.3 34.7 %copy-start.2 = (bf16[3,512,1024]{2,1,0:T(8,128)(2,1)S(1)}, bf16[3,512,1024]{2,1,0:T(8,128)(2,1)}, u32[]{:S(2)}) copy-start(bf16[3,512,1024]{2,1,0:T(8,128)(2,1)} %param.13) | copy-start | bytes 9437188
  46.7 5.9 %copy-start.3 = (s32[4,64]{1,0:T(4,128)S(1)}, s32[4,64]{1,0:T(4,128)}, u32[]{:S(2)}) copy-start(s32[4,64]{1,0:T(4,128)} %param.10) | copy-start | bytes 3076
  46.7 6.0 %copy-start.1 = (s32[96]{0:T(128)S(1)}, s32[96]{0:T(128)}, u32[]{:S(2)}) copy-start(s32[96]{0:T(128)} %param.12) | copy-start | bytes 1156
  47.9 18.9 %all-to-all-start = ((f32[32,4,3,512]{3,1,2,0:T(4,128)}), f32[32,4,3,512]{3,1,2,0:T(4,128)S(1)}, u32[]{:S(2)}, u32[]{:S(2)}) async-start(f32[32,4,3,512]{3,1,2,0:T(4,128)} %copy.25), calls=%async_computation | async-start | bytes 1572864 | tf_op jit(solution)/shard_map/all_to_all | solution.py:91
  54.9 1.9 copy-start.4
  233.8 164.7 %all-to-all-start.1 = ((f32[256,4,503]{2,1,0:T(4,128)}), f32[256,4,503]{2,1,0:T(4,128)S(1)}, u32[]{:S(2)}, u32[]{:S(2)}) async-start(f32[256,4,503]{2,1,0:T(4,128)} %copy.28), calls=%async_computation.1 | async-start | bytes 4194304 | tf_op jit(solution)/shard_map/all_to_all | solution.py:110
Sparse Core Ops, SparseCore 0:
  11.0 122.0 all-gather.4

commit v5 on v4

--- a/solution.py
+++ b/solution.py
@@ -30,7 +30,7 @@
             acc[pl.ds(row, 1), :] = acc[pl.ds(row, 1), :] + jnp.where(lane == (token & 127), weight, 0.0)
         return carry
 
-    lax.fori_loop(0, tok_ref.shape[1], body, 0, unroll=8)
+    lax.fori_loop(0, tok_ref.shape[1], body, 0, unroll=32)
 
     @pl.when(step == pl.num_programs(0) - 1)
     def _():

time: 417 us -> 407 us (0.976)
  Pallas kernels: 298 us -> 288 us
    pallas_call x2, Pallas kernels: 298 us -> 288 us  [knn_scatter(): pl.pallas_call(knn_kernel, grid=(probes,), in_specs=[pl.BlockSpec((rows,...]
  transfers between devices with their start and end apart: 3 -> 3, of which waited for: 1 -> 1; matrix products, arithmetic and copies ran while one was open for 6% -> 6% of each run, Pallas kernels for 72% -> 71%
where the time goes in v5:
time: 407 us
  Pallas kernels  288 us (71%)
  blocking collectives  29.3 us (7%)
  local copies, waits for them, and re-layouts  22.2 us (5%)
  starting transfers between devices  15.5 us (4%)
  other arithmetic  14.4 us (4%)
  between operations  13.6 us (3%)
  matrix products  13.2 us (3%)
  waiting for transfers between devices  10.6 us (3%)
    pallas_call x2, Pallas kernels, knn_scatter(): pl.pallas_call(knn_kernel, grid=(probes,), in_specs=[pl.BlockSpec((rows,...  288 us
    all_gather x1, blocking collectives, shards(): group_queries = lax.all_gather(queries, 'keys', axis=0, tiled=True)  29.3 us
    all_to_all x1, starting transfers between devices, shards(): got = lax.all_to_all(payload, both, split_axis=0, concat_axis=0, tiled=True)  10.9 us
    dot_general x1, matrix products, shards(): jnp.einsum('dri,ic->drc', gathered, head_weight, preferred_element_type=j...  10.1 us
    all_to_all x1, waiting for transfers between devices, shards(): lax.all_to_all(outgoing, 'keys', split_axis=0, concat_axis=2, tiled=True)  9.9 us
  transfers between devices with their start and end apart: 3, of which 1 were waited for; matrix products, arithmetic and copies ran while one was open for 6% of the time, Pallas kernels for 71%

profile of v5, /device:TPU:1, one launch (start us, length us, event | category | flops | bytes accessed | tf_op | source)
XLA Modules:
  0.0 406.7 jit_solution(1375441412822387226)
XLA Ops:
  6.5 0.7 all-gather.5.cloned.1.call-update
  7.3 29.3 %all-gather.1 = bf16[32,4,1024]{2,1,0:T(4,128)(2,1)} all-gather(bf16[1,4,1024]{2,1,0:T(4,128)(2,1)} %bitcast.68), channel_id=1, replica_groups=mesh['keys'=32,'vocab'=8] {'keys'}, dimensions={0}, use_global_device_ids=true | all-gather | bytes 270336 | tf_op jit(solution)/shard_map/all_gather | solution.py:80
  36.6 1.7 reshape.130
  38.3 2.6 multiply_reduce_fusion
  40.9 1.1 multiply_reduce_fusion.1
  42.0 3.0 fusion.5
  45.0 1.7 reshape.97
  46.7 1.2 copy.25
  47.9 4.6 %all-to-all-start = ((f32[32,4,3,512]{3,1,2,0:T(4,128)}), f32[32,4,3,512]{3,1,2,0:T(4,128)S(1)}, u32[]{:S(2)}, u32[]{:S(2)}) async-start(f32[32,4,3,512]{3,1,2,0:T(4,128)} %copy.25), calls=%async_computation | async-start | bytes 1572864 | tf_op jit(solution)/shard_map/all_to_all | solution.py:91
  52.6 1.9 gather_fusion
  54.9 1.0 gather_fusion.1
  55.9 0.9 copy.37
  56.9 9.9 %all-to-all-done = f32[32,4,3,512]{3,1,2,0:T(4,128)S(1)} async-done(((f32[32,4,3,512]{3,1,2,0:T(4,128)}), f32[32,4,3,512]{3,1,2,0:T(4,128)S(1)}, u32[]{:S(2)}, u32[]{:S(2)}) %all-to-all-start) | async-done | bytes 786464 | tf_op jit(solution)/shard_map/all_to_all | solution.py:91
  66.8 0.3 copy.26
  67.0 2.1 gather_fusion.2
  69.4 0.3 fusion.11
  69.9 0.9 copy.38
  70.8 1.5 broadcast_in_dim.56.init_ref
  72.3 144.0 %shard_map.82.init_ref = f32[4,1002,128]{2,1,0:T(8,128)} custom-call(s32[4,16384]{1,0:T(4,128)} %bitcast.63, f32[4,16384]{1,0:T(4,128)} %bitcast.65, f32[4,1002,128]{2,1,0:T(8,128)} %broadcast_in_dim.56.init_ref), custom_call_target="tpu_custom_call", output_to_operand_aliasing={{}: (2, {})} | custom-call | flops 33554432 | bytes 71213056 | tf_op jit(solution)/shard_map/pallas_call | solution.py:46
  216.3 10.1 %fusion.16 = (f32[256,4]{0,1:T(4,128)S(1)}, f32[256,4,501]{0,2,1:T(8,128)S(1)}) fusion(bf16[4096,501]{0,1:T(8,128)(2,1)} %param.15, bf16[256,4,4096]{2,1,0:T(4,128)(2,1)} %all-gather.5.cloned.1.call-done), kind=kOutput, calls=%fused_computation.46 | convolution fusion | flops 4203204608 | bytes 14548992 | tf_op jit(solution)/shard_map/dri,ic->drc/dot_general | solution.py:104
  226.5 0.3 exponential_reduce_fusion
  226.9 2.0 copy.28
  228.9 10.9 %all-to-all-start.1 = ((f32[256,4,503]{2,1,0:T(4,128)}), f32[256,4,503]{2,1,0:T(4,128)S(1)}, u32[]{:S(2)}, u32[]{:S(2)}) async-start(f32[256,4,503]{2,1,0:T(4,128)} %copy.28), calls=%async_computation.1 | async-start | bytes 4194304 | tf_op jit(solution)/shard_map/all_to_all | solution.py:110
  239.8 0.9 copy.35
  240.7 0.9 copy.36
  241.6 144.0 %shard_map.83 = f32[4,1002,128]{2,1,0:T(8,128)} custom-call(s32[4,16384]{1,0:T(4,128)} %bitcast.64, f32[4,16384]{1,0:T(4,128)} %bitcast.66, f32[4,1002,128]{2,1,0:T(8,128)} %shard_map.82.init_ref), custom_call_target="tpu_custom_call", output_to_operand_aliasing={{}: (2, {})} | custom-call | flops 33554432 | bytes 71213056 | tf_op jit(solution)/shard_map/pallas_call | solution.py:46
  385.6 3.1 multiply_bitcast_fusion
  388.8 0.7 fusion.15
  390.3 0.8 fusion.8
  391.1 0.7 copy.32
  391.8 3.5 mul.37
  395.3 4.6 %fusion.9 = f32[4,128256]{1,0:T(4,128)} fusion(f32[4,128256]{1,0:T(4,128)} %mul.37, f32[1,4,1002,128]{3,2,1,0:T(8,128)} %multiply_bitcast_fusion), kind=kLoop, calls=%fused_computation.19 | loop fusion | flops 513024 | bytes 6156288 | tf_op jit(solution)/shard_map/log | solution.py:120
  (37 shorter events, 2.0 us)
Async XLA Ops:
  6.5 48.3 %copy-start = (s32[96,512]{1,0:T(8,128)S(1)}, s32[96,512]{1,0:T(8,128)}, u32[]{:S(2)}) copy-start(s32[96,512]{1,0:T(8,128)} %param.14) | copy-start | bytes 589828
  6.5 209.8 %all-gather.5.cloned.1.call-start = ((), (), s32[]{:S(2)}) async-start(), calls=%async_computation.2 | async-start | bytes 8421376 | tf_op jit(solution)/shard_map/all_gather | solution.py:102
  7.3 34.7 %copy-start.2 = (bf16[3,512,1024]{2,1,0:T(8,128)(2,1)S(1)}, bf16[3,512,1024]{2,1,0:T(8,128)(2,1)}, u32[]{:S(2)}) copy-start(bf16[3,512,1024]{2,1,0:T(8,128)(2,1)} %param.13) | copy-start | bytes 9437188
  46.7 5.9 %copy-start.3 = (s32[4,64]{1,0:T(4,128)S(1)}, s32[4,64]{1,0:T(4,128)}, u32[]{:S(2)}) copy-start(s32[4,64]{1,0:T(4,128)} %param.10) | copy-start | bytes 3076
  46.7 6.0 %copy-start.1 = (s32[96]{0:T(128)S(1)}, s32[96]{0:T(128)}, u32[]{:S(2)}) copy-start(s32[96]{0:T(128)} %param.12) | copy-start | bytes 1156
  47.9 18.9 %all-to-all-start = ((f32[32,4,3,512]{3,1,2,0:T(4,128)}), f32[32,4,3,512]{3,1,2,0:T(4,128)S(1)}, u32[]{:S(2)}, u32[]{:S(2)}) async-start(f32[32,4,3,512]{3,1,2,0:T(4,128)} %copy.25), calls=%async_computation | async-start | bytes 1572864 | tf_op jit(solution)/shard_map/all_to_all | solution.py:91
  54.9 1.9 copy-start.4
  228.9 159.8 %all-to-all-start.1 = ((f32[256,4,503]{2,1,0:T(4,128)}), f32[256,4,503]{2,1,0:T(4,128)S(1)}, u32[]{:S(2)}, u32[]{:S(2)}) async-start(f32[256,4,503]{2,1,0:T(4,128)} %copy.28), calls=%async_computation.1 | async-start | bytes 4194304 | tf_op jit(solution)/shard_map/all_to_all | solution.py:110
Sparse Core Ops, SparseCore 0:
  11.0 122.0 all-gather.4

commit v6 on v5

--- a/solution.py
+++ b/solution.py
@@ -12,7 +12,7 @@
 LANES = 128
 
 
-def knn_kernel(tok_ref, w_ref, init_ref, out_ref, *accs):
+def knn_kernel(line_ref, lane_ref, w_ref, init_ref, out_ref, *accs):
     step = pl.program_id(0)
 
     @pl.when(step == 0)
@@ -24,13 +24,13 @@
 
     def body(i, carry):
         for r, acc in enumerate(accs):
-            token = tok_ref[r, i]
+            row = line_ref[r, i]
+            place = lane_ref[r, i]
             weight = w_ref[r, i]
-            row = token >> 7
-            acc[pl.ds(row, 1), :] = acc[pl.ds(row, 1), :] + jnp.where(lane == (token & 127), weight, 0.0)
+            acc[pl.ds(row, 1), :] = acc[pl.ds(row, 1), :] + jnp.where(lane == place, weight, 0.0)
         return carry
 
-    lax.fori_loop(0, tok_ref.shape[1], body, 0, unroll=32)
+    lax.fori_loop(0, line_ref.shape[1], body, 0, unroll=32)
 
     @pl.when(step == pl.num_programs(0) - 1)
     def _():
@@ -49,6 +49,7 @@
         in_specs=[
             pl.BlockSpec((rows, block_len), lambda j: (0, j), memory_space=pltpu.SMEM),
             pl.BlockSpec((rows, block_len), lambda j: (0, j), memory_space=pltpu.SMEM),
+            pl.BlockSpec((rows, block_len), lambda j: (0, j), memory_space=pltpu.SMEM),
             pl.BlockSpec((rows, lane_rows, LANES), lambda j: (0, 0, 0)),
         ],
         out_specs=pl.BlockSpec((rows, lane_rows, LANES), lambda j: (0, 0, 0)),
@@ -59,8 +60,8 @@
             transcendentals=0,
             bytes_accessed=rows * probes * block_len * LANES * 8 + 8 * rows * lane_rows * LANES,
         ),
-        input_output_aliases={2: 0},
-    )(tok, w, init)
+        input_output_aliases={3: 0},
+    )(tok >> 7, tok & (LANES - 1), w, init)
     return out
 
 

time: 407 us -> 368 us (0.904)
  Pallas kernels: 288 us -> 248 us
    pallas_call x2, Pallas kernels: 288 us -> 248 us  [knn_scatter(): pl.pallas_call(knn_kernel, grid=(probes,), in_specs=[pl.BlockSpec((rows,...]
  transfers between devices with their start and end apart: 3 -> 3, of which waited for: 1 -> 1; matrix products, arithmetic and copies ran while one was open for 6% -> 8% of each run, Pallas kernels for 71% -> 67%
where the time goes in v6:
time: 368 us; the launch traced here: 367 us
  Pallas kernels  248 us (67%)
  blocking collectives  29.3 us (8%)
  local copies, waits for them, and re-layouts  23.9 us (6%)
  starting transfers between devices  15.5 us (4%)
  other arithmetic  14.5 us (4%)
  between operations  13.6 us (4%)
  matrix products  13.2 us (4%)
  waiting for transfers between devices  9.63 us (3%)
    pallas_call x2, Pallas kernels, knn_scatter(): pl.pallas_call(knn_kernel, grid=(probes,), in_specs=[pl.BlockSpec((rows,...  248 us
    all_gather x1, blocking collectives, shards(): group_queries = lax.all_gather(queries, 'keys', axis=0, tiled=True)  29.3 us
    all_to_all x1, starting transfers between devices, shards(): got = lax.all_to_all(payload, both, split_axis=0, concat_axis=0, tiled=True)  10.9 us
    dot_general x1, matrix products, shards(): jnp.einsum('dri,ic->drc', gathered, head_weight, preferred_element_type=j...  10.1 us
    all_to_all x1, waiting for transfers between devices, shards(): lax.all_to_all(outgoing, 'keys', split_axis=0, concat_axis=2, tiled=True)  8.91 us
  transfers between devices with their start and end apart: 3, of which 1 were waited for; matrix products, arithmetic and copies ran while one was open for 8% of the time, Pallas kernels for 67%

profile of v6, /device:TPU:1, one launch (start us, length us, event | category | flops | bytes accessed | tf_op | source)
XLA Modules:
  0.0 367.3 jit_solution(12314038346049954004)
XLA Ops:
  6.5 0.7 all-gather.5.cloned.1.call-update
  7.3 29.3 %all-gather.1 = bf16[32,4,1024]{2,1,0:T(4,128)(2,1)} all-gather(bf16[1,4,1024]{2,1,0:T(4,128)(2,1)} %bitcast.76), channel_id=1, replica_groups=mesh['keys'=32,'vocab'=8] {'keys'}, dimensions={0}, use_global_device_ids=true | all-gather | bytes 270336 | tf_op jit(solution)/shard_map/all_gather | solution.py:81
  36.6 1.7 reshape.132
  38.3 2.6 multiply_reduce_fusion
  40.9 1.1 multiply_reduce_fusion.1
  42.0 3.0 fusion.5
  45.0 1.7 reshape.100
  46.7 1.2 copy.25
  47.9 4.6 %all-to-all-start = ((f32[32,4,3,512]{3,1,2,0:T(4,128)}), f32[32,4,3,512]{3,1,2,0:T(4,128)S(1)}, u32[]{:S(2)}, u32[]{:S(2)}) async-start(f32[32,4,3,512]{3,1,2,0:T(4,128)} %copy.25), calls=%async_computation | async-start | bytes 1572864 | tf_op jit(solution)/shard_map/all_to_all | solution.py:92
  52.6 1.9 gather_fusion
  54.9 1.0 gather_fusion.1
  56.0 0.9 copy.38
  56.9 0.9 copy.39
  57.8 8.9 %all-to-all-done = f32[32,4,3,512]{3,1,2,0:T(4,128)S(1)} async-done(((f32[32,4,3,512]{3,1,2,0:T(4,128)}), f32[32,4,3,512]{3,1,2,0:T(4,128)S(1)}, u32[]{:S(2)}, u32[]{:S(2)}) %all-to-all-start) | async-done | bytes 786464 | tf_op jit(solution)/shard_map/all_to_all | solution.py:92
  67.0 2.1 gather_fusion.2
  69.4 0.3 fusion.11
  69.9 0.9 copy.40
  70.8 1.5 broadcast_in_dim.56.init_ref
  72.3 123.9 %shard_map.82.init_ref = f32[4,1002,128]{2,1,0:T(8,128)} custom-call(s32[4,16384]{1,0:T(4,128)} %bitcast.69, s32[4,16384]{1,0:T(4,128)} %bitcast.70, f32[4,16384]{1,0:T(4,128)} %bitcast.73, f32[4,1002,128]{2,1,0:T(8,128)} %broadcast_in_dim.56.init_ref), custom_call_target="tpu_custom_call", output_to_operand_aliasing={{}: (3, {})} | custom-call | flops 33554432 | bytes 71213056 | tf_op jit(solution)/shard_map/pallas_call | solution.py:46
  196.2 10.1 %fusion.16 = (f32[256,4]{0,1:T(4,128)S(1)}, f32[256,4,501]{0,2,1:T(8,128)S(1)}) fusion(bf16[4096,501]{0,1:T(8,128)(2,1)} %param.15, bf16[256,4,4096]{2,1,0:T(4,128)(2,1)} %all-gather.5.cloned.1.call-done), kind=kOutput, calls=%fused_computation.48 | convolution fusion | flops 4203204608 | bytes 14548992 | tf_op jit(solution)/shard_map/dri,ic->drc/dot_general | solution.py:105
  206.8 2.0 copy.28
  208.8 10.9 %all-to-all-start.1 = ((f32[256,4,503]{2,1,0:T(4,128)}), f32[256,4,503]{2,1,0:T(4,128)S(1)}, u32[]{:S(2)}, u32[]{:S(2)}) async-start(f32[256,4,503]{2,1,0:T(4,128)} %copy.28), calls=%async_computation.1 | async-start | bytes 4194304 | tf_op jit(solution)/shard_map/all_to_all | solution.py:111
  219.7 0.9 copy.35
  220.6 0.9 copy.36
  221.5 0.9 copy.37
  222.3 123.9 %shard_map.83 = f32[4,1002,128]{2,1,0:T(8,128)} custom-call(s32[4,16384]{1,0:T(4,128)} %bitcast.71, s32[4,16384]{1,0:T(4,128)} %bitcast.72, f32[4,16384]{1,0:T(4,128)} %bitcast.74, f32[4,1002,128]{2,1,0:T(8,128)} %shard_map.82.init_ref), custom_call_target="tpu_custom_call", output_to_operand_aliasing={{}: (3, {})} | custom-call | flops 33554432 | bytes 71213056 | tf_op jit(solution)/shard_map/pallas_call | solution.py:46
  346.2 3.1 multiply_bitcast_fusion
  349.4 0.7 fusion.15
  350.9 0.8 fusion.8
  351.7 0.7 copy.32
  352.4 3.5 mul.37
  355.9 4.6 %fusion.9 = f32[4,128256]{1,0:T(4,128)} fusion(f32[4,128256]{1,0:T(4,128)} %mul.37, f32[1,4,1002,128]{3,2,1,0:T(8,128)} %multiply_bitcast_fusion), kind=kLoop, calls=%fused_computation.19 | loop fusion | flops 513024 | bytes 6156288 | tf_op jit(solution)/shard_map/log | solution.py:121
  (39 shorter events, 2.7 us)
Async XLA Ops:
  6.5 48.3 %copy-start = (s32[96,512]{1,0:T(8,128)S(1)}, s32[96,512]{1,0:T(8,128)}, u32[]{:S(2)}) copy-start(s32[96,512]{1,0:T(8,128)} %param.14) | copy-start | bytes 589828
  6.5 189.6 %all-gather.5.cloned.1.call-start = ((), (), s32[]{:S(2)}) async-start(), calls=%async_computation.2 | async-start | bytes 8421376 | tf_op jit(solution)/shard_map/all_gather | solution.py:103
  7.3 34.7 %copy-start.2 = (bf16[3,512,1024]{2,1,0:T(8,128)(2,1)S(1)}, bf16[3,512,1024]{2,1,0:T(8,128)(2,1)}, u32[]{:S(2)}) copy-start(bf16[3,512,1024]{2,1,0:T(8,128)(2,1)} %param.13) | copy-start | bytes 9437188
  46.7 5.9 %copy-start.3 = (s32[4,64]{1,0:T(4,128)S(1)}, s32[4,64]{1,0:T(4,128)}, u32[]{:S(2)}) copy-start(s32[4,64]{1,0:T(4,128)} %param.10) | copy-start | bytes 3076
  46.7 6.0 %copy-start.1 = (s32[96]{0:T(128)S(1)}, s32[96]{0:T(128)}, u32[]{:S(2)}) copy-start(s32[96]{0:T(128)} %param.12) | copy-start | bytes 1156
  47.9 18.9 %all-to-all-start = ((f32[32,4,3,512]{3,1,2,0:T(4,128)}), f32[32,4,3,512]{3,1,2,0:T(4,128)S(1)}, u32[]{:S(2)}, u32[]{:S(2)}) async-start(f32[32,4,3,512]{3,1,2,0:T(4,128)} %copy.25), calls=%async_computation | async-start | bytes 1572864 | tf_op jit(solution)/shard_map/all_to_all | solution.py:92
  55.8 1.9 copy-start.4
  208.8 140.5 %all-to-all-start.1 = ((f32[256,4,503]{2,1,0:T(4,128)}), f32[256,4,503]{2,1,0:T(4,128)S(1)}, u32[]{:S(2)}, u32[]{:S(2)}) async-start(f32[256,4,503]{2,1,0:T(4,128)} %copy.28), calls=%async_computation.1 | async-start | bytes 4194304 | tf_op jit(solution)/shard_map/all_to_all | solution.py:111
Sparse Core Ops, SparseCore 0:
  11.0 122.0 all-gather.4

commit v7 on v6

--- a/solution.py
+++ b/solution.py
@@ -106,11 +106,12 @@
     local_peak = jnp.max(logits, axis=2, keepdims=True)
     shifted = logits - local_peak
     local_sum = jnp.sum(jnp.exp(shifted), axis=2, keepdims=True)
-    payload = jnp.concatenate([shifted, local_peak, local_sum], axis=2)
+    spare = jnp.zeros(shifted.shape[:2] + (LANES - (piece_cols + 2) % LANES,), jnp.float32)
+    payload = jnp.concatenate([shifted, local_peak, local_sum, spare], axis=2)
     payload, knn_first = lax.optimization_barrier((payload, knn_first))
     got = lax.all_to_all(payload, both, split_axis=0, concat_axis=0, tiled=True)
     knn_mass = knn_scatter(tokens[:, half:], weights[:, half:], knn_first).reshape(rows_dev, vocab_size)
-    got = got.reshape(devices, rows_dev, piece_cols + 2)
+    got = got.reshape(devices, rows_dev, payload.shape[2])
     piece_peak = got[:, :, piece_cols]
     row_peak = jnp.max(piece_peak, axis=0)
     row_sum = jnp.sum(got[:, :, piece_cols + 1] * jnp.exp(piece_peak - row_peak[None, :]), axis=0)

time: 368 us -> 368 us (level)
  no operation moved by 1% of the time
where the time goes in v7:
time: 368 us; the launch traced here: 367 us
  Pallas kernels  248 us (67%)
  blocking collectives  29.3 us (8%)
  local copies, waits for them, and re-layouts  24 us (7%)
  starting transfers between devices  15.5 us (4%)
  other arithmetic  14.6 us (4%)
  between operations  13.6 us (4%)
  matrix products  13.2 us (4%)
  waiting for transfers between devices  9.55 us (3%)
    pallas_call x2, Pallas kernels, knn_scatter(): pl.pallas_call(knn_kernel, grid=(probes,), in_specs=[pl.BlockSpec((rows,...  248 us
    all_gather x1, blocking collectives, shards(): group_queries = lax.all_gather(queries, 'keys', axis=0, tiled=True)  29.3 us
    all_to_all x1, starting transfers between devices, shards(): got = lax.all_to_all(payload, both, split_axis=0, concat_axis=0, tiled=True)  10.9 us
    dot_general x1, matrix products, shards(): jnp.einsum('dri,ic->drc', gathered, head_weight, preferred_element_type=j...  10.1 us
    all_to_all x1, waiting for transfers between devices, shards(): lax.all_to_all(outgoing, 'keys', split_axis=0, concat_axis=2, tiled=True)  8.83 us
  transfers between devices with their start and end apart: 3, of which 1 were waited for; matrix products, arithmetic and copies ran while one was open for 8% of the time, Pallas kernels for 67%

profile of v7, /device:TPU:1, one launch (start us, length us, event | category | flops | bytes accessed | tf_op | source)
XLA Modules:
  0.0 367.4 jit_solution(8386074305001898547)
XLA Ops:
  6.5 0.7 all-gather.5.cloned.1.call-update
  7.3 29.3 %all-gather.1 = bf16[32,4,1024]{2,1,0:T(4,128)(2,1)} all-gather(bf16[1,4,1024]{2,1,0:T(4,128)(2,1)} %bitcast.76), channel_id=1, replica_groups=mesh['keys'=32,'vocab'=8] {'keys'}, dimensions={0}, use_global_device_ids=true | all-gather | bytes 270336 | tf_op jit(solution)/shard_map/all_gather | solution.py:81
  36.6 1.7 reshape.132
  38.3 2.6 multiply_reduce_fusion
  40.9 1.1 multiply_reduce_fusion.1
  42.0 3.0 fusion.5
  45.0 1.7 reshape.100
  46.7 1.2 copy.25
  47.9 4.6 %all-to-all-start = ((f32[32,4,3,512]{3,1,2,0:T(4,128)}), f32[32,4,3,512]{3,1,2,0:T(4,128)S(1)}, u32[]{:S(2)}, u32[]{:S(2)}) async-start(f32[32,4,3,512]{3,1,2,0:T(4,128)} %copy.25), calls=%async_computation | async-start | bytes 1572864 | tf_op jit(solution)/shard_map/all_to_all | solution.py:92
  52.6 1.9 gather_fusion
  54.9 1.0 gather_fusion.1
  56.0 0.9 copy.38
  56.9 0.9 copy.39
  57.9 8.8 %all-to-all-done = f32[32,4,3,512]{3,1,2,0:T(4,128)S(1)} async-done(((f32[32,4,3,512]{3,1,2,0:T(4,128)}), f32[32,4,3,512]{3,1,2,0:T(4,128)S(1)}, u32[]{:S(2)}, u32[]{:S(2)}) %all-to-all-start) | async-done | bytes 786464 | tf_op jit(solution)/shard_map/all_to_all | solution.py:92
  67.0 2.1 gather_fusion.2
  69.4 0.3 fusion.11
  69.9 0.9 copy.40
  70.8 1.5 broadcast_in_dim.59.init_ref
  72.3 123.9 %shard_map.82.init_ref = f32[4,1002,128]{2,1,0:T(8,128)} custom-call(s32[4,16384]{1,0:T(4,128)} %bitcast.69, s32[4,16384]{1,0:T(4,128)} %bitcast.70, f32[4,16384]{1,0:T(4,128)} %bitcast.73, f32[4,1002,128]{2,1,0:T(8,128)} %broadcast_in_dim.59.init_ref), custom_call_target="tpu_custom_call", output_to_operand_aliasing={{}: (3, {})} | custom-call | flops 33554432 | bytes 71213056 | tf_op jit(solution)/shard_map/pallas_call | solution.py:46
  196.2 10.1 %fusion.16 = (f32[256,4]{0,1:T(4,128)S(1)}, f32[256,4,501]{0,2,1:T(8,128)S(1)}) fusion(bf16[4096,501]{0,1:T(8,128)(2,1)} %param.15, bf16[256,4,4096]{2,1,0:T(4,128)(2,1)} %all-gather.5.cloned.1.call-done), kind=kOutput, calls=%fused_computation.48 | convolution fusion | flops 4203204608 | bytes 14548992 | tf_op jit(solution)/shard_map/dri,ic->drc/dot_general | solution.py:105
  206.9 2.0 copy.28
  208.9 10.9 %all-to-all-start.1 = ((f32[256,4,512]{2,1,0:T(4,128)}), f32[256,4,512]{2,1,0:T(4,128)S(1)}, u32[]{:S(2)}, u32[]{:S(2)}) async-start(f32[256,4,512]{2,1,0:T(4,128)} %copy.28), calls=%async_computation.1 | async-start | bytes 4194304 | tf_op jit(solution)/shard_map/all_to_all | solution.py:112
  219.8 0.9 copy.35
  220.7 0.9 copy.36
  221.5 0.9 copy.37
  222.4 123.9 %shard_map.83 = f32[4,1002,128]{2,1,0:T(8,128)} custom-call(s32[4,16384]{1,0:T(4,128)} %bitcast.71, s32[4,16384]{1,0:T(4,128)} %bitcast.72, f32[4,16384]{1,0:T(4,128)} %bitcast.74, f32[4,1002,128]{2,1,0:T(8,128)} %shard_map.82.init_ref), custom_call_target="tpu_custom_call", output_to_operand_aliasing={{}: (3, {})} | custom-call | flops 33554432 | bytes 71213056 | tf_op jit(solution)/shard_map/pallas_call | solution.py:46
  346.3 3.1 multiply_bitcast_fusion
  349.5 0.7 fusion.15
  351.0 0.8 fusion.8
  351.8 0.7 copy.32
  352.5 3.5 mul.37
  356.0 4.6 %fusion.9 = f32[4,128256]{1,0:T(4,128)} fusion(f32[4,128256]{1,0:T(4,128)} %mul.37, f32[1,4,1002,128]{3,2,1,0:T(8,128)} %multiply_bitcast_fusion), kind=kLoop, calls=%fused_computation.19 | loop fusion | flops 513024 | bytes 6156288 | tf_op jit(solution)/shard_map/log | solution.py:122
  (41 shorter events, 2.8 us)
Async XLA Ops:
  6.5 48.3 %copy-start = (s32[96,512]{1,0:T(8,128)S(1)}, s32[96,512]{1,0:T(8,128)}, u32[]{:S(2)}) copy-start(s32[96,512]{1,0:T(8,128)} %param.14) | copy-start | bytes 589828
  6.5 189.6 %all-gather.5.cloned.1.call-start = ((), (), s32[]{:S(2)}) async-start(), calls=%async_computation.2 | async-start | bytes 8421376 | tf_op jit(solution)/shard_map/all_gather | solution.py:103
  7.3 34.7 %copy-start.2 = (bf16[3,512,1024]{2,1,0:T(8,128)(2,1)S(1)}, bf16[3,512,1024]{2,1,0:T(8,128)(2,1)}, u32[]{:S(2)}) copy-start(bf16[3,512,1024]{2,1,0:T(8,128)(2,1)} %param.13) | copy-start | bytes 9437188
  46.7 5.9 %copy-start.3 = (s32[4,64]{1,0:T(4,128)S(1)}, s32[4,64]{1,0:T(4,128)}, u32[]{:S(2)}) copy-start(s32[4,64]{1,0:T(4,128)} %param.10) | copy-start | bytes 3076
  46.7 6.0 %copy-start.1 = (s32[96]{0:T(128)S(1)}, s32[96]{0:T(128)}, u32[]{:S(2)}) copy-start(s32[96]{0:T(128)} %param.12) | copy-start | bytes 1156
  47.9 18.9 %all-to-all-start = ((f32[32,4,3,512]{3,1,2,0:T(4,128)}), f32[32,4,3,512]{3,1,2,0:T(4,128)S(1)}, u32[]{:S(2)}, u32[]{:S(2)}) async-start(f32[32,4,3,512]{3,1,2,0:T(4,128)} %copy.25), calls=%async_computation | async-start | bytes 1572864 | tf_op jit(solution)/shard_map/all_to_all | solution.py:92
  55.8 2.0 copy-start.4
  208.9 140.6 %all-to-all-start.1 = ((f32[256,4,512]{2,1,0:T(4,128)}), f32[256,4,512]{2,1,0:T(4,128)S(1)}, u32[]{:S(2)}, u32[]{:S(2)}) async-start(f32[256,4,512]{2,1,0:T(4,128)} %copy.28), calls=%async_computation.1 | async-start | bytes 4194304 | tf_op jit(solution)/shard_map/all_to_all | solution.py:112
Sparse Core Ops, SparseCore 0:
  11.0 122.0 all-gather.4

commit v8 on v7

--- a/solution.py
+++ b/solution.py
@@ -30,7 +30,7 @@
             acc[pl.ds(row, 1), :] = acc[pl.ds(row, 1), :] + jnp.where(lane == place, weight, 0.0)
         return carry
 
-    lax.fori_loop(0, line_ref.shape[1], body, 0, unroll=32)
+    lax.fori_loop(0, line_ref.shape[1], body, 0, unroll=64)
 
     @pl.when(step == pl.num_programs(0) - 1)
     def _():

time: 368 us -> 365 us (level)
  no operation moved by 1% of the time
where the time goes in v8:
time: 365 us; the launch traced here: 364 us
  Pallas kernels  245 us (67%)
  blocking collectives  29.3 us (8%)
  local copies, waits for them, and re-layouts  24 us (7%)
  starting transfers between devices  15.5 us (4%)
  other arithmetic  14.6 us (4%)
  between operations  13.6 us (4%)
  matrix products  13.2 us (4%)
  waiting for transfers between devices  9.55 us (3%)
    pallas_call x2, Pallas kernels, knn_scatter(): pl.pallas_call(knn_kernel, grid=(probes,), in_specs=[pl.BlockSpec((rows,...  245 us
    all_gather x1, blocking collectives, shards(): group_queries = lax.all_gather(queries, 'keys', axis=0, tiled=True)  29.3 us
    all_to_all x1, starting transfers between devices, shards(): got = lax.all_to_all(payload, both, split_axis=0, concat_axis=0, tiled=True)  10.9 us
    dot_general x1, matrix products, shards(): jnp.einsum('dri,ic->drc', gathered, head_weight, preferred_element_type=j...  10.2 us
    all_to_all x1, waiting for transfers between devices, shards(): lax.all_to_all(outgoing, 'keys', split_axis=0, concat_axis=2, tiled=True)  8.83 us
  transfers between devices with their start and end apart: 3, of which 1 were waited for; matrix products, arithmetic and copies ran while one was open for 8% of the time, Pallas kernels for 67%

profile of v8, /device:TPU:1, one launch (start us, length us, event | category | flops | bytes accessed | tf_op | source)
XLA Modules:
  0.0 364.5 jit_solution(10303639051100690324)
XLA Ops:
  6.5 0.7 all-gather.5.cloned.1.call-update
  7.3 29.3 %all-gather.1 = bf16[32,4,1024]{2,1,0:T(4,128)(2,1)} all-gather(bf16[1,4,1024]{2,1,0:T(4,128)(2,1)} %bitcast.76), channel_id=1, replica_groups=mesh['keys'=32,'vocab'=8] {'keys'}, dimensions={0}, use_global_device_ids=true | all-gather | bytes 270336 | tf_op jit(solution)/shard_map/all_gather | solution.py:81
  36.6 1.7 reshape.132
  38.3 2.6 multiply_reduce_fusion
  40.9 1.1 multiply_reduce_fusion.1
  42.0 3.0 fusion.5
  45.0 1.7 reshape.100
  46.7 1.2 copy.25
  47.9 4.6 %all-to-all-start = ((f32[32,4,3,512]{3,1,2,0:T(4,128)}), f32[32,4,3,512]{3,1,2,0:T(4,128)S(1)}, u32[]{:S(2)}, u32[]{:S(2)}) async-start(f32[32,4,3,512]{3,1,2,0:T(4,128)} %copy.25), calls=%async_computation | async-start | bytes 1572864 | tf_op jit(solution)/shard_map/all_to_all | solution.py:92
  52.6 1.9 gather_fusion
  54.9 1.0 gather_fusion.1
  56.0 0.9 copy.38
  56.9 0.9 copy.39
  57.9 8.8 %all-to-all-done = f32[32,4,3,512]{3,1,2,0:T(4,128)S(1)} async-done(((f32[32,4,3,512]{3,1,2,0:T(4,128)}), f32[32,4,3,512]{3,1,2,0:T(4,128)S(1)}, u32[]{:S(2)}, u32[]{:S(2)}) %all-to-all-start) | async-done | bytes 786464 | tf_op jit(solution)/shard_map/all_to_all | solution.py:92
  67.0 2.1 gather_fusion.2
  69.4 0.3 fusion.11
  69.9 0.9 copy.40
  70.8 1.5 broadcast_in_dim.59.init_ref
  72.3 122.4 %shard_map.82.init_ref = f32[4,1002,128]{2,1,0:T(8,128)} custom-call(s32[4,16384]{1,0:T(4,128)} %bitcast.69, s32[4,16384]{1,0:T(4,128)} %bitcast.70, f32[4,16384]{1,0:T(4,128)} %bitcast.73, f32[4,1002,128]{2,1,0:T(8,128)} %broadcast_in_dim.59.init_ref), custom_call_target="tpu_custom_call", output_to_operand_aliasing={{}: (3, {})} | custom-call | flops 33554432 | bytes 71213056 | tf_op jit(solution)/shard_map/pallas_call | solution.py:46
  194.7 10.2 %fusion.16 = (f32[256,4]{0,1:T(4,128)S(1)}, f32[256,4,501]{0,2,1:T(8,128)S(1)}) fusion(bf16[4096,501]{0,1:T(8,128)(2,1)} %param.15, bf16[256,4,4096]{2,1,0:T(4,128)(2,1)} %all-gather.5.cloned.1.call-done), kind=kOutput, calls=%fused_computation.48 | convolution fusion | flops 4203204608 | bytes 14548992 | tf_op jit(solution)/shard_map/dri,ic->drc/dot_general | solution.py:105
  205.4 2.0 copy.28
  207.4 10.9 %all-to-all-start.1 = ((f32[256,4,512]{2,1,0:T(4,128)}), f32[256,4,512]{2,1,0:T(4,128)S(1)}, u32[]{:S(2)}, u32[]{:S(2)}) async-start(f32[256,4,512]{2,1,0:T(4,128)} %copy.28), calls=%async_computation.1 | async-start | bytes 4194304 | tf_op jit(solution)/shard_map/all_to_all | solution.py:112
  218.3 0.9 copy.35
  219.2 0.9 copy.36
  220.1 0.9 copy.37
  220.9 122.4 %shard_map.83 = f32[4,1002,128]{2,1,0:T(8,128)} custom-call(s32[4,16384]{1,0:T(4,128)} %bitcast.71, s32[4,16384]{1,0:T(4,128)} %bitcast.72, f32[4,16384]{1,0:T(4,128)} %bitcast.74, f32[4,1002,128]{2,1,0:T(8,128)} %shard_map.82.init_ref), custom_call_target="tpu_custom_call", output_to_operand_aliasing={{}: (3, {})} | custom-call | flops 33554432 | bytes 71213056 | tf_op jit(solution)/shard_map/pallas_call | solution.py:46
  343.4 3.1 multiply_bitcast_fusion
  346.5 0.7 fusion.15
  348.0 0.8 fusion.8
  348.8 0.7 copy.32
  349.5 3.5 mul.37
  353.0 4.6 %fusion.9 = f32[4,128256]{1,0:T(4,128)} fusion(f32[4,128256]{1,0:T(4,128)} %mul.37, f32[1,4,1002,128]{3,2,1,0:T(8,128)} %multiply_bitcast_fusion), kind=kLoop, calls=%fused_computation.19 | loop fusion | flops 513024 | bytes 6156288 | tf_op jit(solution)/shard_map/log | solution.py:122
  (41 shorter events, 2.8 us)
Async XLA Ops:
  6.5 48.3 %copy-start = (s32[96,512]{1,0:T(8,128)S(1)}, s32[96,512]{1,0:T(8,128)}, u32[]{:S(2)}) copy-start(s32[96,512]{1,0:T(8,128)} %param.14) | copy-start | bytes 589828
  6.5 188.2 %all-gather.5.cloned.1.call-start = ((), (), s32[]{:S(2)}) async-start(), calls=%async_computation.2 | async-start | bytes 8421376 | tf_op jit(solution)/shard_map/all_gather | solution.py:103
  7.3 34.7 %copy-start.2 = (bf16[3,512,1024]{2,1,0:T(8,128)(2,1)S(1)}, bf16[3,512,1024]{2,1,0:T(8,128)(2,1)}, u32[]{:S(2)}) copy-start(bf16[3,512,1024]{2,1,0:T(8,128)(2,1)} %param.13) | copy-start | bytes 9437188
  46.7 5.9 %copy-start.3 = (s32[4,64]{1,0:T(4,128)S(1)}, s32[4,64]{1,0:T(4,128)}, u32[]{:S(2)}) copy-start(s32[4,64]{1,0:T(4,128)} %param.10) | copy-start | bytes 3076
  46.7 6.0 %copy-start.1 = (s32[96]{0:T(128)S(1)}, s32[96]{0:T(128)}, u32[]{:S(2)}) copy-start(s32[96]{0:T(128)} %param.12) | copy-start | bytes 1156
  47.9 18.9 %all-to-all-start = ((f32[32,4,3,512]{3,1,2,0:T(4,128)}), f32[32,4,3,512]{3,1,2,0:T(4,128)S(1)}, u32[]{:S(2)}, u32[]{:S(2)}) async-start(f32[32,4,3,512]{3,1,2,0:T(4,128)} %copy.25), calls=%async_computation | async-start | bytes 1572864 | tf_op jit(solution)/shard_map/all_to_all | solution.py:92
  55.8 2.0 copy-start.4
  207.4 139.1 %all-to-all-start.1 = ((f32[256,4,512]{2,1,0:T(4,128)}), f32[256,4,512]{2,1,0:T(4,128)S(1)}, u32[]{:S(2)}, u32[]{:S(2)}) async-start(f32[256,4,512]{2,1,0:T(4,128)} %copy.28), calls=%async_computation.1 | async-start | bytes 4194304 | tf_op jit(solution)/shard_map/all_to_all | solution.py:112
Sparse Core Ops, SparseCore 0:
  11.0 122.0 all-gather.4
